TPU v7x, 128 devices: a whole 4x4x4 slice. The times are simulated.
128 devices in a mesh: seg: 16 (over x, y_lo, core), dp: 8 (over y_hi, z).
Axes of the slice: x: 4, y: 4 (y_hi: 2, y_lo: 2; y = y_hi * 2 + y_lo), z: 4, core: 2. Of those that a mesh axis runs over, the one named last changes fastest.
Arguments:
- hidden: bfloat16 [8, 5120, 4096], P('dp', 'seg'), may hold values from -6 to 6
- norm_gain: bfloat16 [4096], replicated, may hold values from 0.5 to 1.5
- value_weight: bfloat16 [4096, 2048], replicated, may hold values from -0.09375 to 0.09375
- queries: bfloat16 [8, 5120, 2048], P('dp', 'seg'), may hold values from -100 to 100
- token_keys: bfloat16 [8, 5120, 2048], P('dp', 'seg'), may hold values from -5 to 5
- summary_keys: bfloat16 [8, 800, 2048], P('dp', 'seg'), may hold values from -5 to 5
- output_grad: bfloat16 [8, 5120, 2048], P('dp', 'seg'), may hold values from -6 to 6
Outputs:
- grad_hidden: bfloat16 [8, 5120, 4096], P('dp', 'seg')
- summary_grads: float32 [8, 800, 2048], P('dp', 'seg')
- grad_weight: float32 [4096, 2048], P(('seg', 'dp'))
- grad_gain: float32 [4096], P(('seg', 'dp'))
All inputs are finite; a program needn't handle non-finite values.
Results may differ from a plain program's by a relative error of at most 0.0058.
Values sent between devices are 32-bit elements; how exact they have to be, the bound alone decides.
No kernel may reach another device: no remote copies, remote signals or barrier semaphores. Data moves between devices by JAX's collectives and lax.ppermute only.
A program may use at most 192 MiB of HBM per device.

v0:
```python
import jax
import jax.numpy as jnp
from jax import lax
from jax.sharding import PartitionSpec as P

HEADS = 16
HEAD_DIM = 128


def passed_along(block, axis, distance):
    devices = range(lax.axis_size(axis))
    route = [(i - distance, i) for i in devices if i - distance in devices]
    return lax.ppermute(block, axis, route)


def mixing_of(query_rows, key_rows, summary_rows):
    trace_count, row_count, value_width = query_rows.shape
    slot_count = summary_rows.shape[1]
    query_heads = query_rows.reshape(trace_count, row_count, HEADS, HEAD_DIM)
    all_keys = jnp.concatenate([summary_rows, key_rows], axis=1)
    all_keys = all_keys.reshape(trace_count, slot_count + row_count, HEADS, HEAD_DIM)
    scores = jnp.einsum(
        "trhd,tkhd->thrk", query_heads, all_keys, preferred_element_type=jnp.float32
    )
    scores = scores * HEAD_DIM ** (-0.5)
    row_pos = lax.broadcasted_iota(jnp.int32, (row_count, slot_count + row_count), 0)
    col_pos = lax.broadcasted_iota(jnp.int32, (row_count, slot_count + row_count), 1)
    scores = jnp.where(col_pos <= row_pos + slot_count, scores, jnp.float32(-1e30))
    row_peak = jnp.max(scores, axis=-1, keepdims=True)
    exp_scores = jnp.exp(scores - row_peak)
    return (exp_scores / jnp.sum(exp_scores, axis=-1, keepdims=True)).astype(jnp.bfloat16)


def apply_map(matrix, state):
    return jnp.einsum("thkr,trhd->tkhd", matrix, state, precision=lax.Precision.HIGHEST)


def local(hidden, norm_gain, value_weight, queries, token_keys, summary_keys, output_grad):
    trace_count, row_count, value_width = queries.shape
    slot_count = summary_keys.shape[1]
    model_width = hidden.shape[2]
    mixing = mixing_of(queries, token_keys, summary_keys)
    grad_heads = output_grad.reshape(trace_count, row_count, HEADS, HEAD_DIM)
    direct = jnp.einsum("thrk,trhd->tkhd", mixing, grad_heads, preferred_element_type=jnp.float32)
    slot_mixing = mixing[:, :, row_count - slot_count :, :].astype(jnp.float32)
    own_map = jnp.swapaxes(slot_mixing[..., :slot_count], 2, 3)
    own_offset = direct[:, :slot_count]

    def advance(incoming):
        return apply_map(own_map, incoming) + own_offset

    def one_step(turn_index, incoming):
        outgoing = advance(incoming).reshape(trace_count, slot_count, value_width)
        arrived = passed_along(outgoing, "seg", -1)
        return arrived.reshape(trace_count, slot_count, HEADS, HEAD_DIM)

    start_state = jnp.zeros((trace_count, slot_count, HEADS, HEAD_DIM), jnp.float32)
    incoming = lax.fori_loop(0, lax.axis_size("seg") - 1, one_step, start_state)
    summary_grad = advance(incoming).reshape(trace_count, slot_count, value_width)
    token_part = jnp.einsum(
        "thrk,trhd->tkhd", slot_mixing[..., slot_count:], incoming, precision=lax.Precision.HIGHEST
    )
    value_grad = (direct[:, slot_count:] + token_part).astype(jnp.bfloat16)
    value_grad = value_grad.reshape(trace_count * row_count, value_width)
    hidden_f = hidden.astype(jnp.float32)
    inv_rms = lax.rsqrt(jnp.mean(hidden_f * hidden_f, axis=-1, keepdims=True) + 1e-05)
    normed = hidden_f * inv_rms
    gain_f = norm_gain.astype(jnp.float32)
    scaled = (normed * gain_f).astype(jnp.bfloat16).reshape(trace_count * row_count, model_width)
    weight_grad = lax.dot_general(
        scaled, value_grad, (((0,), (0,)), ((), ())), preferred_element_type=jnp.float32
    )
    normalized_gradient = lax.dot_general(
        value_grad, value_weight, (((1,), (1,)), ((), ())), preferred_element_type=jnp.float32
    )
    normalized_gradient = normalized_gradient.reshape(trace_count, row_count, model_width)
    gain_grad = jnp.sum(
        (normalized_gradient * normed).reshape(trace_count * row_count, model_width), axis=0
    )
    scaled_grad = normalized_gradient * gain_f
    hidden_grad = inv_rms * (
        scaled_grad - normed * jnp.mean(scaled_grad * normed, axis=-1, keepdims=True)
    )
    weight_part, gain_part = (
        lax.psum_scatter(weight_grad, ("seg", "dp"), scatter_dimension=0, tiled=True),
        lax.psum_scatter(gain_grad, ("seg", "dp"), scatter_dimension=0, tiled=True),
    )
    return (hidden_grad.astype(jnp.bfloat16), summary_grad, weight_part, gain_part)


def solution(mesh):
    placed = (
        P("dp", "seg", None),
        P(),
        P(),
        P("dp", "seg", None),
        P("dp", "seg", None),
        P("dp", "seg", None),
        P("dp", "seg", None),
    )
    return jax.shard_map(
        local,
        mesh=mesh,
        in_specs=placed,
        out_specs=(
            P("dp", "seg", None),
            P("dp", "seg", None),
            P(("seg", "dp"), None),
            P(("seg", "dp")),
        ),
        check_vma=False,
    )
```

profile of v0, /device:TPU:0, one launch (start us, length us, event | category | flops | bytes accessed | tf_op | source)
XLA Modules:
  0.0 936.8 jit_solution(17746772443750515776)
XLA Ops:
  7.3 2.5 fusion.15
  10.6 2.7 copy.44
  13.3 1.4 copy.45
  15.0 0.9 copy.32
  15.9 2.5 fusion.29
  18.4 4.6 fusion.40
  22.9 0.9 fusion.44
  24.2 4.4 convolution_bitcast_fusion.1
  29.0 1.1 slice.23
  30.1 154.1 %while.10 = (s32[]{:T(128)}, f32[1,50,16,128]{3,2,0,1:T(8,128)S(1)}, f32[1,16,50,50]{3,2,1,0:T(8,128)S(1)}, f32[1,50,16,128]{3,1,2,0:T(8,128)S(1)}, s32[]{:T(128)}) while((s32[]{:T(128)}, f32[1,50,16,128]{3,2,0,1:T(8,128)S(1)}, f32[1,16,50,50]{3,2,1,0:T(8,128)S(1)}, f32[1,50,16,128]{3,1,2,0:T(8,128)S(1)}, s32[]{:T(128)}) %tuple.28), condition=%wide.region_4.5_spmd, body=%wide.region_3.4_spmd.sunk | while | flops 61542400 | bytes 3846501 | solution.py:58
  30.1 1.0 fusion.50
  31.2 1.3 collective-permute-start
  32.5 2.3 collective-permute-done
  34.8 1.0 fusion.50
  36.0 1.3 collective-permute-start
  37.3 7.5 collective-permute-done
  44.8 1.0 fusion.50
  45.9 1.3 collective-permute-start
  47.2 8.0 collective-permute-done
  55.2 1.0 fusion.50
  56.3 1.3 collective-permute-start
  57.6 8.0 collective-permute-done
  65.5 1.0 fusion.50
  66.7 1.3 collective-permute-start
  68.0 8.0 collective-permute-done
  75.9 1.0 fusion.50
  77.0 1.3 collective-permute-start
  78.3 8.0 collective-permute-done
  86.3 1.0 fusion.50
  87.4 1.3 collective-permute-start
  88.7 8.0 collective-permute-done
  96.7 1.0 fusion.50
  97.8 1.3 collective-permute-start
  99.1 8.0 collective-permute-done
  107.1 1.0 fusion.50
  108.2 1.3 collective-permute-start
  109.5 8.0 collective-permute-done
  117.5 1.0 fusion.50
  118.6 1.3 collective-permute-start
  119.9 8.0 collective-permute-done
  127.8 1.0 fusion.50
  129.0 1.3 collective-permute-start
  130.3 8.8 collective-permute-done
  139.1 1.0 fusion.50
  140.2 1.3 collective-permute-start
  141.5 8.9 collective-permute-done
  150.4 1.0 fusion.50
  151.5 1.3 collective-permute-start
  152.8 8.9 collective-permute-done
  161.7 1.0 fusion.50
  162.8 1.3 collective-permute-start
  164.1 8.9 collective-permute-done
  172.9 1.0 fusion.50
  174.0 1.3 collective-permute-start
  175.3 8.9 collective-permute-done
  184.2 4.3 fusion.22
  188.5 0.8 copy.38
  189.4 1.0 copy-done.1
  190.5 15.4 %fusion.20 = f32[4096,2048]{1,0:T(8,128)} fusion(bf16[1,320,4096]{2,1,0:T(8,128)(2,1)S(1)} %copy-done, f32[4096]{0:T(1024)S(1)} %convert_element_type.26, f32[320]{0:T(512)S(1)} %add_rsqrt_fusion, bf16[40,8,16,128]{3,2,1,0:T(8,128)(2,1)S(1)} %bitcast.95), kind=kOutput, calls=%fused_computation.26 | convolution fusion | flops 5373952000 | bytes 37504256 | tf_op jit(solution)/shard_map/dot_general | solution.py:70
  205.9 1.8 fusion.31
  208.5 11.7 %fusion.14 = (f32[4096]{0:T(1024)S(1)}, f32[320]{0:T(512)S(1)}, f32[320,4096]{1,0:T(8,128)}) fusion(bf16[1,320,4096]{2,1,0:T(8,128)(2,1)S(1)} %copy-done, f32[320]{0:T(512)S(1)} %add_rsqrt_fusion, f32[4096]{0:T(1024)S(1)} %convert_element_type.26, bf16[4096,2048]{1,0:T(8,128)(2,1)} %param.11, bf16[40,8,16,128]{3,2,1,0:T(8,128)(2,1)} %bitcast.96), kind=kOutput, calls=%fused_computation.20 | convolution fusion | flops 5377879552 | bytes 25987584 | tf_op jit(solution)/shard_map/dot_general | solution.py:73
  220.1 92.3 %all-reduce = f32[4096]{0:T(1024)S(1)} all-reduce(f32[4096]{0:T(1024)S(1)} %get-tuple-element.39), channel_id=3, replica_groups=mesh['seg'=16,'dp'=8] {'seg','dp'}, use_global_device_ids=true, to_apply=%region_8.9.clone | all-reduce | flops 4096 | bytes 32768
  313.1 5.4 fusion.12
  318.5 611.4 %reduce-scatter.2.cloned.1.call-done = f32[32,2048]{1,0:T(8,128)} async-done(((f32[4096,2048]{1,0:T(8,128)}), f32[32,2048]{1,0:T(8,128)}) %reduce-scatter.2.cloned.1.call-update) | async-done | bytes 262160 | tf_op jit(solution)/shard_map/reduce_scatter | solution.py:85
  (41 shorter events, 4.7 us)
Async XLA Ops:
  7.2 6.1 copy-start.3
  7.2 922.7 %reduce-scatter.2.cloned.1.call-start = ((), (), s32[]{:S(2)}) async-start(), calls=%async_computation.1 | async-start | bytes 33816576 | tf_op jit(solution)/shard_map/reduce_scatter | solution.py:85
  7.2 7.4 copy-start.4
  7.2 7.4 copy-start.6
  22.9 1.3 copy-start.5
  23.8 4.9 copy-start.2
  31.2 3.6 collective-permute-start
  36.0 8.8 collective-permute-start
  45.9 9.3 collective-permute-start
  56.3 9.3 collective-permute-start
  66.7 9.3 collective-permute-start
  77.0 9.3 collective-permute-start
  87.4 9.3 collective-permute-start
  97.8 9.3 collective-permute-start
  108.2 9.3 collective-permute-start
  118.6 9.3 collective-permute-start
  129.0 10.1 %collective-permute-start = (f32[1,50,2048]{2,0,1:T(1,128)S(1)}, f32[1,50,2048]{2,0,1:T(1,128)S(1)}, u32[]{:S(2)}, u32[]{:S(2)}) collective-permute-start(f32[1,50,2048]{2,0,1:T(1,128)S(1)} %bitcast.92), channel_id=1, source_target_pairs={{8,0},{16,8},{24,16},{32,24},{40,32},{48,40},{56,48},{64,56},{72,6... | collective-permute-start | bytes 1228808 | tf_op jit(solution)/shard_map/while/body/eval_jaxpr/ppermute | solution.py:13
  140.2 10.2 %collective-permute-start = (f32[1,50,2048]{2,0,1:T(1,128)S(1)}, f32[1,50,2048]{2,0,1:T(1,128)S(1)}, u32[]{:S(2)}, u32[]{:S(2)}) collective-permute-start(f32[1,50,2048]{2,0,1:T(1,128)S(1)} %bitcast.92), channel_id=1, source_target_pairs={{8,0},{16,8},{24,16},{32,24},{40,32},{48,40},{56,48},{64,56},{72,6... | collective-permute-start | bytes 1228808 | tf_op jit(solution)/shard_map/while/body/eval_jaxpr/ppermute | solution.py:13
  151.5 10.2 %collective-permute-start = (f32[1,50,2048]{2,0,1:T(1,128)S(1)}, f32[1,50,2048]{2,0,1:T(1,128)S(1)}, u32[]{:S(2)}, u32[]{:S(2)}) collective-permute-start(f32[1,50,2048]{2,0,1:T(1,128)S(1)} %bitcast.92), channel_id=1, source_target_pairs={{8,0},{16,8},{24,16},{32,24},{40,32},{48,40},{56,48},{64,56},{72,6... | collective-permute-start | bytes 1228808 | tf_op jit(solution)/shard_map/while/body/eval_jaxpr/ppermute | solution.py:13
  162.8 10.2 %collective-permute-start = (f32[1,50,2048]{2,0,1:T(1,128)S(1)}, f32[1,50,2048]{2,0,1:T(1,128)S(1)}, u32[]{:S(2)}, u32[]{:S(2)}) collective-permute-start(f32[1,50,2048]{2,0,1:T(1,128)S(1)} %bitcast.92), channel_id=1, source_target_pairs={{8,0},{16,8},{24,16},{32,24},{40,32},{48,40},{56,48},{64,56},{72,6... | collective-permute-start | bytes 1228808 | tf_op jit(solution)/shard_map/while/body/eval_jaxpr/ppermute | solution.py:13
  174.0 10.2 %collective-permute-start = (f32[1,50,2048]{2,0,1:T(1,128)S(1)}, f32[1,50,2048]{2,0,1:T(1,128)S(1)}, u32[]{:S(2)}, u32[]{:S(2)}) collective-permute-start(f32[1,50,2048]{2,0,1:T(1,128)S(1)} %bitcast.92), channel_id=1, source_target_pairs={{8,0},{16,8},{24,16},{32,24},{40,32},{48,40},{56,48},{64,56},{72,6... | collective-permute-start | bytes 1228808 | tf_op jit(solution)/shard_map/while/body/eval_jaxpr/ppermute | solution.py:13
  184.2 6.2 copy-start
  189.4 1.1 copy-start.1
Sparse Core Ops, SparseCore 0:
  206.0 723.8 reduce-scatter.1
where the time goes:
time: 938 us; the launch traced here: 937 us
  waiting for transfers between devices  729 us (78%)
  blocking collectives  92.3 us (10%)
  matrix products  55.2 us (6%)
  starting transfers between devices  19.4 us (2%)
  other arithmetic  14.6 us (2%)
  between operations  14.2 us (2%)
  local copies, waits for them, and re-layouts  11.2 us (1%)
    reduce_scatter x1, waiting for transfers between devices, local(): lax.psum_scatter(weight_grad, ('seg', 'dp'), scatter_dimension=0, tiled=T...  611 us
    ppermute x15, waiting for transfers between devices, passed_along(): return lax.ppermute(block, axis, route)  118 us
    unnamed x1, blocking collectives  92.3 us
    ppermute x15, starting transfers between devices, passed_along(): return lax.ppermute(block, axis, route)  19.4 us
  transfers between devices with their start and end apart: 16, of which 16 were waited for; matrix products, arithmetic and copies ran while one was open for 2% of the time, Pallas kernels for 0%

commit v1 on v0

--- a/solution.py
+++ b/solution.py
@@ -81,10 +81,11 @@
     hidden_grad = inv_rms * (
         scaled_grad - normed * jnp.mean(scaled_grad * normed, axis=-1, keepdims=True)
     )
-    weight_part, gain_part = (
-        lax.psum_scatter(weight_grad, ("seg", "dp"), scatter_dimension=0, tiled=True),
-        lax.psum_scatter(gain_grad, ("seg", "dp"), scatter_dimension=0, tiled=True),
-    )
+    gain_block = jnp.zeros((model_width, 128), jnp.float32).at[:, 0].set(gain_grad)
+    both = jnp.concatenate([weight_grad, gain_block], axis=1)
+    both = lax.psum_scatter(both, "seg", scatter_dimension=0, tiled=True)
+    both = lax.psum_scatter(both, "dp", scatter_dimension=0, tiled=True)
+    weight_part, gain_part = both[:, :value_width], both[:, value_width]
     return (hidden_grad.astype(jnp.bfloat16), summary_grad, weight_part, gain_part)
 
 

time: 938 us -> 719 us (0.77)
  waiting for transfers between devices: 729 us -> 574 us
  blocking collectives: 92.3 us -> 0 us
  other arithmetic: 14.6 us -> 39.3 us
    reduce_scatter x1, waiting for transfers between devices: 611 us -> 382 us  [local(): both = lax.psum_scatter(both, 'seg', scatter_dimension=0, tiled=True)]
    unnamed x1 -> x0, blocking collectives: 92.3 us -> none
    unnamed x1 -> x3, waiting for transfers between devices: 0.02 us -> 73.8 us
    concatenate x0 -> x1, other arithmetic: none -> 23.4 us  [local(): both = jnp.concatenate([weight_grad, gain_block], axis=1)]
  transfers between devices with their start and end apart: 16 -> 17, of which waited for: 16 -> 17; matrix products, arithmetic and copies ran while one was open for 2% -> 1% of each run, Pallas kernels for 0% -> 0%
where the time goes in v1:
time: 719 us; the launch traced here: 718 us
  waiting for transfers between devices  574 us (80%)
  matrix products  55.2 us (8%)
  other arithmetic  39.3 us (5%)
  starting transfers between devices  19.5 us (3%)
  local copies, waits for them, and re-layouts  15.6 us (2%)
  between operations  14.2 us (2%)
    reduce_scatter x1, waiting for transfers between devices, local(): both = lax.psum_scatter(both, 'seg', scatter_dimension=0, tiled=True)  382 us
    ppermute x15, waiting for transfers between devices, passed_along(): return lax.ppermute(block, axis, route)  118 us
    unnamed x3, waiting for transfers between devices  73.8 us
    concatenate x1, other arithmetic, local(): both = jnp.concatenate([weight_grad, gain_block], axis=1)  23.4 us
    ppermute x15, starting transfers between devices, passed_along(): return lax.ppermute(block, axis, route)  19.4 us
    dot_general x16, matrix products, apply_map(): jnp.einsum('thkr,trhd->tkhd', matrix, state, precision=lax.Precision.HIGH...  16.9 us
    dot_general x1, matrix products, local(): lax.dot_general(scaled, value_grad, (((0,), (0,)), ((), ())), preferred_e...  15.6 us
  transfers between devices with their start and end apart: 17, of which 17 were waited for; matrix products, arithmetic and copies ran while one was open for 1% of the time, Pallas kernels for 0%

profile of v1, /device:TPU:0, one launch (start us, length us, event | category | flops | bytes accessed | tf_op | source)
XLA Modules:
  0.0 718.2 jit_solution(13830366122462088414)
XLA Ops:
  7.9 2.5 fusion.15
  11.2 2.7 copy.51
  13.9 1.4 copy.52
  16.4 2.5 fusion.29
  18.9 4.6 fusion.40
  23.5 0.9 fusion.44
  24.8 4.5 convolution_bitcast_fusion.1
  29.6 1.1 slice.45
  30.7 154.1 %while.11 = (s32[]{:T(128)}, f32[1,50,16,128]{3,2,0,1:T(8,128)S(1)}, f32[1,16,50,50]{3,2,1,0:T(8,128)S(1)}, f32[1,50,16,128]{3,1,2,0:T(8,128)S(1)}, s32[]{:T(128)}) while((s32[]{:T(128)}, f32[1,50,16,128]{3,2,0,1:T(8,128)S(1)}, f32[1,16,50,50]{3,2,1,0:T(8,128)S(1)}, f32[1,50,16,128]{3,1,2,0:T(8,128)S(1)}, s32[]{:T(128)}) %tuple.35), condition=%wide.region_4.5_spmd, body=%wide.region_3.4_spmd.sunk | while | flops 61542400 | bytes 3846501 | solution.py:58
  30.7 1.0 fusion.50
  31.8 1.3 collective-permute-start
  33.1 2.3 collective-permute-done
  35.5 1.0 fusion.50
  36.6 1.3 collective-permute-start
  37.9 7.5 %collective-permute-done = f32[1,50,2048]{2,0,1:T(1,128)S(1)} collective-permute-done((f32[1,50,2048]{2,0,1:T(1,128)S(1)}, f32[1,50,2048]{2,0,1:T(1,128)S(1)}, u32[]{:S(2)}, u32[]{:S(2)}) %collective-permute-start) | collective-permute-done | bytes 409632 | tf_op jit(solution)/shard_map/while/body/eval_jaxpr/ppermute | solution.py:13
  45.4 1.0 fusion.50
  46.5 1.3 collective-permute-start
  47.8 8.0 %collective-permute-done = f32[1,50,2048]{2,0,1:T(1,128)S(1)} collective-permute-done((f32[1,50,2048]{2,0,1:T(1,128)S(1)}, f32[1,50,2048]{2,0,1:T(1,128)S(1)}, u32[]{:S(2)}, u32[]{:S(2)}) %collective-permute-start) | collective-permute-done | bytes 409632 | tf_op jit(solution)/shard_map/while/body/eval_jaxpr/ppermute | solution.py:13
  55.8 1.0 fusion.50
  56.9 1.3 collective-permute-start
  58.2 8.0 %collective-permute-done = f32[1,50,2048]{2,0,1:T(1,128)S(1)} collective-permute-done((f32[1,50,2048]{2,0,1:T(1,128)S(1)}, f32[1,50,2048]{2,0,1:T(1,128)S(1)}, u32[]{:S(2)}, u32[]{:S(2)}) %collective-permute-start) | collective-permute-done | bytes 409632 | tf_op jit(solution)/shard_map/while/body/eval_jaxpr/ppermute | solution.py:13
  66.2 1.0 fusion.50
  67.3 1.3 collective-permute-start
  68.6 8.0 %collective-permute-done = f32[1,50,2048]{2,0,1:T(1,128)S(1)} collective-permute-done((f32[1,50,2048]{2,0,1:T(1,128)S(1)}, f32[1,50,2048]{2,0,1:T(1,128)S(1)}, u32[]{:S(2)}, u32[]{:S(2)}) %collective-permute-start) | collective-permute-done | bytes 409632 | tf_op jit(solution)/shard_map/while/body/eval_jaxpr/ppermute | solution.py:13
  76.5 1.0 fusion.50
  77.6 1.3 collective-permute-start
  79.0 8.0 %collective-permute-done = f32[1,50,2048]{2,0,1:T(1,128)S(1)} collective-permute-done((f32[1,50,2048]{2,0,1:T(1,128)S(1)}, f32[1,50,2048]{2,0,1:T(1,128)S(1)}, u32[]{:S(2)}, u32[]{:S(2)}) %collective-permute-start) | collective-permute-done | bytes 409632 | tf_op jit(solution)/shard_map/while/body/eval_jaxpr/ppermute | solution.py:13
  86.9 1.0 fusion.50
  88.0 1.3 collective-permute-start
  89.3 8.0 %collective-permute-done = f32[1,50,2048]{2,0,1:T(1,128)S(1)} collective-permute-done((f32[1,50,2048]{2,0,1:T(1,128)S(1)}, f32[1,50,2048]{2,0,1:T(1,128)S(1)}, u32[]{:S(2)}, u32[]{:S(2)}) %collective-permute-start) | collective-permute-done | bytes 409632 | tf_op jit(solution)/shard_map/while/body/eval_jaxpr/ppermute | solution.py:13
  97.3 1.0 fusion.50
  98.4 1.3 collective-permute-start
  99.7 8.0 %collective-permute-done = f32[1,50,2048]{2,0,1:T(1,128)S(1)} collective-permute-done((f32[1,50,2048]{2,0,1:T(1,128)S(1)}, f32[1,50,2048]{2,0,1:T(1,128)S(1)}, u32[]{:S(2)}, u32[]{:S(2)}) %collective-permute-start) | collective-permute-done | bytes 409632 | tf_op jit(solution)/shard_map/while/body/eval_jaxpr/ppermute | solution.py:13
  107.7 1.0 fusion.50
  108.8 1.3 collective-permute-start
  110.1 8.0 %collective-permute-done = f32[1,50,2048]{2,0,1:T(1,128)S(1)} collective-permute-done((f32[1,50,2048]{2,0,1:T(1,128)S(1)}, f32[1,50,2048]{2,0,1:T(1,128)S(1)}, u32[]{:S(2)}, u32[]{:S(2)}) %collective-permute-start) | collective-permute-done | bytes 409632 | tf_op jit(solution)/shard_map/while/body/eval_jaxpr/ppermute | solution.py:13
  118.1 1.0 fusion.50
  119.2 1.3 collective-permute-start
  120.5 8.0 %collective-permute-done = f32[1,50,2048]{2,0,1:T(1,128)S(1)} collective-permute-done((f32[1,50,2048]{2,0,1:T(1,128)S(1)}, f32[1,50,2048]{2,0,1:T(1,128)S(1)}, u32[]{:S(2)}, u32[]{:S(2)}) %collective-permute-start) | collective-permute-done | bytes 409632 | tf_op jit(solution)/shard_map/while/body/eval_jaxpr/ppermute | solution.py:13
  128.5 1.0 fusion.50
  129.6 1.3 collective-permute-start
  130.9 8.9 %collective-permute-done = f32[1,50,2048]{2,0,1:T(1,128)S(1)} collective-permute-done((f32[1,50,2048]{2,0,1:T(1,128)S(1)}, f32[1,50,2048]{2,0,1:T(1,128)S(1)}, u32[]{:S(2)}, u32[]{:S(2)}) %collective-permute-start) | collective-permute-done | bytes 409632 | tf_op jit(solution)/shard_map/while/body/eval_jaxpr/ppermute | solution.py:13
  139.7 1.0 fusion.50
  140.8 1.3 collective-permute-start
  142.1 8.9 %collective-permute-done = f32[1,50,2048]{2,0,1:T(1,128)S(1)} collective-permute-done((f32[1,50,2048]{2,0,1:T(1,128)S(1)}, f32[1,50,2048]{2,0,1:T(1,128)S(1)}, u32[]{:S(2)}, u32[]{:S(2)}) %collective-permute-start) | collective-permute-done | bytes 409632 | tf_op jit(solution)/shard_map/while/body/eval_jaxpr/ppermute | solution.py:13
  151.0 1.0 fusion.50
  152.1 1.3 collective-permute-start
  153.4 8.9 %collective-permute-done = f32[1,50,2048]{2,0,1:T(1,128)S(1)} collective-permute-done((f32[1,50,2048]{2,0,1:T(1,128)S(1)}, f32[1,50,2048]{2,0,1:T(1,128)S(1)}, u32[]{:S(2)}, u32[]{:S(2)}) %collective-permute-start) | collective-permute-done | bytes 409632 | tf_op jit(solution)/shard_map/while/body/eval_jaxpr/ppermute | solution.py:13
  162.3 1.0 fusion.50
  163.4 1.3 collective-permute-start
  164.7 8.9 %collective-permute-done = f32[1,50,2048]{2,0,1:T(1,128)S(1)} collective-permute-done((f32[1,50,2048]{2,0,1:T(1,128)S(1)}, f32[1,50,2048]{2,0,1:T(1,128)S(1)}, u32[]{:S(2)}, u32[]{:S(2)}) %collective-permute-start) | collective-permute-done | bytes 409632 | tf_op jit(solution)/shard_map/while/body/eval_jaxpr/ppermute | solution.py:13
  173.6 1.0 fusion.50
  174.7 1.3 collective-permute-start
  176.0 8.9 %collective-permute-done = f32[1,50,2048]{2,0,1:T(1,128)S(1)} collective-permute-done((f32[1,50,2048]{2,0,1:T(1,128)S(1)}, f32[1,50,2048]{2,0,1:T(1,128)S(1)}, u32[]{:S(2)}, u32[]{:S(2)}) %collective-permute-start) | collective-permute-done | bytes 409632 | tf_op jit(solution)/shard_map/while/body/eval_jaxpr/ppermute | solution.py:13
  184.8 4.3 fusion.22
  190.0 15.6 %fusion.20 = f32[4096,2048]{0,1:T(8,128)} fusion(bf16[1,320,4096]{2,1,0:T(8,128)(2,1)S(1)} %copy-done, f32[4096]{0:T(1024)S(1)} %convert_element_type.26, f32[320]{0:T(512)S(1)} %add_rsqrt_fusion, bf16[40,8,16,128]{3,2,1,0:T(8,128)(2,1)S(1)} %bitcast.98), kind=kOutput, calls=%fused_computation.28 | convolution fusion | flops 5373952000 | bytes 37504256 | tf_op jit(solution)/shard_map/dot_general | solution.py:70
  205.6 11.4 %fusion.14 = (f32[4096]{0:T(1024)S(1)}, f32[320]{0:T(512)S(1)}, f32[320,4096]{1,0:T(8,128)}) fusion(bf16[1,320,4096]{2,1,0:T(8,128)(2,1)S(1)} %copy-done, f32[320]{0:T(512)S(1)} %add_rsqrt_fusion, f32[4096]{0:T(1024)S(1)} %convert_element_type.26, bf16[4096,2048]{1,0:T(8,128)(2,1)} %param.13, bf16[40,8,16,128]{3,2,1,0:T(8,128)(2,1)S(1)} %bitcast.99), kind=kOutput, calls=%fused_computation.22 | convolution fusion | flops 5377879552 | bytes 25987584 | tf_op jit(solution)/shard_map/dot_general | solution.py:73
  217.7 23.4 %select_maximum_fusion = f32[4096,2176]{0,1:T(8,128)} fusion(f32[4096,1]{0,1:T(1,128)S(1)} %bitcast.104, f32[4096,2048]{0,1:T(8,128)} %fusion.20), kind=kLoop, calls=%fused_computation.5 | loop fusion | flops 26738688 | bytes 69222400 | tf_op jit(solution)/shard_map/concatenate | solution.py:85
  241.1 382.4 %reduce-scatter.5.cloned.1.call-done = f32[256,2176]{0,1:T(8,128)} async-done(((f32[4096,2176]{0,1:T(8,128)}), f32[256,2176]{0,1:T(8,128)}) %reduce-scatter.5.cloned.1.call-update) | async-done | bytes 2228240 | tf_op jit(solution)/shard_map/reduce_scatter | solution.py:86
  623.5 3.0 copy.47
  626.6 1.8 fusion.31
  629.2 5.4 fusion.12
  634.7 73.7 %reduce-scatter.7.cloned.1.call-done = f32[32,2176]{1,0:T(8,128)} async-done(((f32[256,2176]{1,0:T(8,128)}), f32[32,2176]{1,0:T(8,128)}) %reduce-scatter.7.cloned.1.call-update) | async-done | bytes 278544
  709.7 1.7 slice.47
  (47 shorter events, 8.4 us)
Async XLA Ops:
  7.2 6.7 copy-start.2
  7.2 8.0 %copy-start.5 = (bf16[1,50,2048]{2,1,0:T(8,128)(2,1)S(1)}, bf16[1,50,2048]{2,1,0:T(8,128)(2,1)}, u32[]{:S(2)}) copy-start(bf16[1,50,2048]{2,1,0:T(8,128)(2,1)} %param.16) | copy-start | bytes 614404
  7.2 616.4 %reduce-scatter.5.cloned.1.call-start = ((), (), s32[]{:S(2)}) async-start(), calls=%async_computation.2 | async-start | bytes 37879808 | tf_op jit(solution)/shard_map/reduce_scatter | solution.py:86
  7.9 7.4 %copy-start.3 = (bf16[1,320,2048]{2,1,0:T(8,128)(2,1)S(1)}, bf16[1,320,2048]{2,1,0:T(8,128)(2,1)}, u32[]{:S(2)}) copy-start(bf16[1,320,2048]{2,1,0:T(8,128)(2,1)} %param.15) | copy-start | bytes 3932164
  23.5 1.3 copy-start.4
  24.4 4.9 copy-start.1
  31.8 3.6 collective-permute-start
  36.6 8.8 %collective-permute-start = (f32[1,50,2048]{2,0,1:T(1,128)S(1)}, f32[1,50,2048]{2,0,1:T(1,128)S(1)}, u32[]{:S(2)}, u32[]{:S(2)}) collective-permute-start(f32[1,50,2048]{2,0,1:T(1,128)S(1)} %bitcast.95), channel_id=1, source_target_pairs={{8,0},{16,8},{24,16},{32,24},{40,32},{48,40},{56,48},{64,56},{72,6... | collective-permute-start | bytes 1228808 | tf_op jit(solution)/shard_map/while/body/eval_jaxpr/ppermute | solution.py:13
  46.5 9.3 %collective-permute-start = (f32[1,50,2048]{2,0,1:T(1,128)S(1)}, f32[1,50,2048]{2,0,1:T(1,128)S(1)}, u32[]{:S(2)}, u32[]{:S(2)}) collective-permute-start(f32[1,50,2048]{2,0,1:T(1,128)S(1)} %bitcast.95), channel_id=1, source_target_pairs={{8,0},{16,8},{24,16},{32,24},{40,32},{48,40},{56,48},{64,56},{72,6... | collective-permute-start | bytes 1228808 | tf_op jit(solution)/shard_map/while/body/eval_jaxpr/ppermute | solution.py:13
  56.9 9.3 %collective-permute-start = (f32[1,50,2048]{2,0,1:T(1,128)S(1)}, f32[1,50,2048]{2,0,1:T(1,128)S(1)}, u32[]{:S(2)}, u32[]{:S(2)}) collective-permute-start(f32[1,50,2048]{2,0,1:T(1,128)S(1)} %bitcast.95), channel_id=1, source_target_pairs={{8,0},{16,8},{24,16},{32,24},{40,32},{48,40},{56,48},{64,56},{72,6... | collective-permute-start | bytes 1228808 | tf_op jit(solution)/shard_map/while/body/eval_jaxpr/ppermute | solution.py:13
  67.3 9.3 %collective-permute-start = (f32[1,50,2048]{2,0,1:T(1,128)S(1)}, f32[1,50,2048]{2,0,1:T(1,128)S(1)}, u32[]{:S(2)}, u32[]{:S(2)}) collective-permute-start(f32[1,50,2048]{2,0,1:T(1,128)S(1)} %bitcast.95), channel_id=1, source_target_pairs={{8,0},{16,8},{24,16},{32,24},{40,32},{48,40},{56,48},{64,56},{72,6... | collective-permute-start | bytes 1228808 | tf_op jit(solution)/shard_map/while/body/eval_jaxpr/ppermute | solution.py:13
  77.6 9.3 %collective-permute-start = (f32[1,50,2048]{2,0,1:T(1,128)S(1)}, f32[1,50,2048]{2,0,1:T(1,128)S(1)}, u32[]{:S(2)}, u32[]{:S(2)}) collective-permute-start(f32[1,50,2048]{2,0,1:T(1,128)S(1)} %bitcast.95), channel_id=1, source_target_pairs={{8,0},{16,8},{24,16},{32,24},{40,32},{48,40},{56,48},{64,56},{72,6... | collective-permute-start | bytes 1228808 | tf_op jit(solution)/shard_map/while/body/eval_jaxpr/ppermute | solution.py:13
  88.0 9.3 %collective-permute-start = (f32[1,50,2048]{2,0,1:T(1,128)S(1)}, f32[1,50,2048]{2,0,1:T(1,128)S(1)}, u32[]{:S(2)}, u32[]{:S(2)}) collective-permute-start(f32[1,50,2048]{2,0,1:T(1,128)S(1)} %bitcast.95), channel_id=1, source_target_pairs={{8,0},{16,8},{24,16},{32,24},{40,32},{48,40},{56,48},{64,56},{72,6... | collective-permute-start | bytes 1228808 | tf_op jit(solution)/shard_map/while/body/eval_jaxpr/ppermute | solution.py:13
  98.4 9.3 %collective-permute-start = (f32[1,50,2048]{2,0,1:T(1,128)S(1)}, f32[1,50,2048]{2,0,1:T(1,128)S(1)}, u32[]{:S(2)}, u32[]{:S(2)}) collective-permute-start(f32[1,50,2048]{2,0,1:T(1,128)S(1)} %bitcast.95), channel_id=1, source_target_pairs={{8,0},{16,8},{24,16},{32,24},{40,32},{48,40},{56,48},{64,56},{72,6... | collective-permute-start | bytes 1228808 | tf_op jit(solution)/shard_map/while/body/eval_jaxpr/ppermute | solution.py:13
  108.8 9.3 %collective-permute-start = (f32[1,50,2048]{2,0,1:T(1,128)S(1)}, f32[1,50,2048]{2,0,1:T(1,128)S(1)}, u32[]{:S(2)}, u32[]{:S(2)}) collective-permute-start(f32[1,50,2048]{2,0,1:T(1,128)S(1)} %bitcast.95), channel_id=1, source_target_pairs={{8,0},{16,8},{24,16},{32,24},{40,32},{48,40},{56,48},{64,56},{72,6... | collective-permute-start | bytes 1228808 | tf_op jit(solution)/shard_map/while/body/eval_jaxpr/ppermute | solution.py:13
  119.2 9.3 %collective-permute-start = (f32[1,50,2048]{2,0,1:T(1,128)S(1)}, f32[1,50,2048]{2,0,1:T(1,128)S(1)}, u32[]{:S(2)}, u32[]{:S(2)}) collective-permute-start(f32[1,50,2048]{2,0,1:T(1,128)S(1)} %bitcast.95), channel_id=1, source_target_pairs={{8,0},{16,8},{24,16},{32,24},{40,32},{48,40},{56,48},{64,56},{72,6... | collective-permute-start | bytes 1228808 | tf_op jit(solution)/shard_map/while/body/eval_jaxpr/ppermute | solution.py:13
  129.6 10.2 %collective-permute-start = (f32[1,50,2048]{2,0,1:T(1,128)S(1)}, f32[1,50,2048]{2,0,1:T(1,128)S(1)}, u32[]{:S(2)}, u32[]{:S(2)}) collective-permute-start(f32[1,50,2048]{2,0,1:T(1,128)S(1)} %bitcast.95), channel_id=1, source_target_pairs={{8,0},{16,8},{24,16},{32,24},{40,32},{48,40},{56,48},{64,56},{72,6... | collective-permute-start | bytes 1228808 | tf_op jit(solution)/shard_map/while/body/eval_jaxpr/ppermute | solution.py:13
  140.8 10.2 %collective-permute-start = (f32[1,50,2048]{2,0,1:T(1,128)S(1)}, f32[1,50,2048]{2,0,1:T(1,128)S(1)}, u32[]{:S(2)}, u32[]{:S(2)}) collective-permute-start(f32[1,50,2048]{2,0,1:T(1,128)S(1)} %bitcast.95), channel_id=1, source_target_pairs={{8,0},{16,8},{24,16},{32,24},{40,32},{48,40},{56,48},{64,56},{72,6... | collective-permute-start | bytes 1228808 | tf_op jit(solution)/shard_map/while/body/eval_jaxpr/ppermute | solution.py:13
  152.1 10.2 %collective-permute-start = (f32[1,50,2048]{2,0,1:T(1,128)S(1)}, f32[1,50,2048]{2,0,1:T(1,128)S(1)}, u32[]{:S(2)}, u32[]{:S(2)}) collective-permute-start(f32[1,50,2048]{2,0,1:T(1,128)S(1)} %bitcast.95), channel_id=1, source_target_pairs={{8,0},{16,8},{24,16},{32,24},{40,32},{48,40},{56,48},{64,56},{72,6... | collective-permute-start | bytes 1228808 | tf_op jit(solution)/shard_map/while/body/eval_jaxpr/ppermute | solution.py:13
  163.4 10.2 %collective-permute-start = (f32[1,50,2048]{2,0,1:T(1,128)S(1)}, f32[1,50,2048]{2,0,1:T(1,128)S(1)}, u32[]{:S(2)}, u32[]{:S(2)}) collective-permute-start(f32[1,50,2048]{2,0,1:T(1,128)S(1)} %bitcast.95), channel_id=1, source_target_pairs={{8,0},{16,8},{24,16},{32,24},{40,32},{48,40},{56,48},{64,56},{72,6... | collective-permute-start | bytes 1228808 | tf_op jit(solution)/shard_map/while/body/eval_jaxpr/ppermute | solution.py:13
  174.7 10.2 %collective-permute-start = (f32[1,50,2048]{2,0,1:T(1,128)S(1)}, f32[1,50,2048]{2,0,1:T(1,128)S(1)}, u32[]{:S(2)}, u32[]{:S(2)}) collective-permute-start(f32[1,50,2048]{2,0,1:T(1,128)S(1)} %bitcast.95), channel_id=1, source_target_pairs={{8,0},{16,8},{24,16},{32,24},{40,32},{48,40},{56,48},{64,56},{72,6... | collective-permute-start | bytes 1228808 | tf_op jit(solution)/shard_map/while/body/eval_jaxpr/ppermute | solution.py:13
  184.8 5.2 copy-start
  241.1 467.3 %reduce-scatter.7.cloned.1.call-start = ((), (), s32[]{:S(2)}) async-start(), calls=%async_computation.3 | async-start | bytes 2506752
Sparse Core Ops, SparseCore 0:
  241.2 382.2 reduce-scatter.4
  627.3 81.0 reduce-scatter.6

commit v2 on v1

--- a/solution.py
+++ b/solution.py
@@ -1,3 +1,4 @@
+import numpy as np
 import jax
 import jax.numpy as jnp
 from jax import lax
@@ -33,6 +34,83 @@
 
 def apply_map(matrix, state):
     return jnp.einsum("thkr,trhd->tkhd", matrix, state, precision=lax.Precision.HIGHEST)
+
+
+def ring_step_perm(size, sign):
+    return [(i, (i + sign) % size) for i in range(size)]
+
+
+def ring_reduce(data, coord, axes, forward, backward):
+    rows, cols = data.shape
+    quarter = data.reshape(4, 2, rows // 8, cols)
+    ahead, behind = quarter[:, 0], quarter[:, 1]
+
+    def own(block, index):
+        return lax.dynamic_index_in_dim(block, index % 4, 0, keepdims=False)
+
+    acc_a = own(ahead, coord - 1)
+    acc_b = own(behind, coord + 1)
+    for step in (2, 3, 4):
+        acc_a = lax.ppermute(acc_a, axes, forward) + own(ahead, coord - step)
+        acc_b = lax.ppermute(acc_b, axes, backward) + own(behind, coord + step)
+    return jnp.concatenate([acc_a, acc_b], axis=0)
+
+
+def shifted(size, move):
+    return [(i, move(i)) for i in range(size)]
+
+
+def reduction_plan(seg_size, dp_size):
+    x_n, z_n = seg_size // 4, dp_size // 2
+
+    def coords(s, d):
+        return {"x": s // 4, "y": 2 * (d // z_n) + (s // 2) % 2, "z": d % z_n, "core": s % 2}
+
+    def linear(s, d):
+        return s * dp_size + d
+
+    def y_move(sign):
+        def move(i):
+            s, d = divmod(i, dp_size)
+            y = (2 * (d // z_n) + (s // 2) % 2 + sign) % 4
+            return linear((s // 4) * 4 + (y % 2) * 2 + s % 2, (y // 2) * z_n + d % z_n)
+        return move
+
+    perms = {
+        "x": [shifted(seg_size, lambda i, g=g: ((i // 4 + g) % x_n) * 4 + i % 4) for g in (1, -1)],
+        "z": [shifted(dp_size, lambda i, g=g: (i // z_n) * z_n + (i % z_n + g) % z_n) for g in (1, -1)],
+        "y": [shifted(seg_size * dp_size, y_move(g)) for g in (1, -1)],
+    }
+    axes = {"x": "seg", "z": "dp", "y": ("seg", "dp")}
+    return coords, perms, axes
+
+
+ORDERS = (("x", "y", "z"), ("y", "z", "x"), ("z", "x", "y"))
+
+
+def row_order(order, seg_size, dp_size, block):
+    coords, _, _ = reduction_plan(seg_size, dp_size)
+    target = {}
+    for s in range(seg_size):
+        for d in range(dp_size):
+            c = coords(s, d)
+            nested = ((c["core"] * 4 + c[order[0]]) * 4 + c[order[1]]) * 4 + c[order[2]]
+            target[nested] = s * dp_size + d
+    return np.concatenate([np.arange(block) + target[n] * block for n in range(len(target))])
+
+
+def reduce_scatter_rows(part, order, where):
+    coords, perms, axes = reduction_plan(lax.axis_size("seg"), lax.axis_size("dp"))
+    rows = part.shape[0]
+    core = where["core"]
+    half = rows // 2
+    send = lax.dynamic_slice_in_dim(part, (1 - core) * half, half, 0)
+    keep = lax.dynamic_slice_in_dim(part, core * half, half, 0)
+    seg_size = lax.axis_size("seg")
+    part = keep + lax.ppermute(send, "seg", shifted(seg_size, lambda i: i ^ 1))
+    for dim in order:
+        part = ring_reduce(part, where[dim], axes[dim], perms[dim][0], perms[dim][1])
+    return part
 
 
 def local(hidden, norm_gain, value_weight, queries, token_keys, summary_keys, output_grad):
@@ -67,9 +145,6 @@
     normed = hidden_f * inv_rms
     gain_f = norm_gain.astype(jnp.float32)
     scaled = (normed * gain_f).astype(jnp.bfloat16).reshape(trace_count * row_count, model_width)
-    weight_grad = lax.dot_general(
-        scaled, value_grad, (((0,), (0,)), ((), ())), preferred_element_type=jnp.float32
-    )
     normalized_gradient = lax.dot_general(
         value_grad, value_weight, (((1,), (1,)), ((), ())), preferred_element_type=jnp.float32
     )
@@ -81,10 +156,29 @@
     hidden_grad = inv_rms * (
         scaled_grad - normed * jnp.mean(scaled_grad * normed, axis=-1, keepdims=True)
     )
-    gain_block = jnp.zeros((model_width, 128), jnp.float32).at[:, 0].set(gain_grad)
-    both = jnp.concatenate([weight_grad, gain_block], axis=1)
-    both = lax.psum_scatter(both, "seg", scatter_dimension=0, tiled=True)
-    both = lax.psum_scatter(both, "dp", scatter_dimension=0, tiled=True)
+    seg_index, dp_index = lax.axis_index("seg"), lax.axis_index("dp")
+    z_n = lax.axis_size("dp") // 2
+    where = {
+        "x": seg_index // 4,
+        "y": 2 * (dp_index // z_n) + (seg_index // 2) % 2,
+        "z": dp_index % z_n,
+        "core": seg_index % 2,
+    }
+    seg_size, dp_size = lax.axis_size("seg"), lax.axis_size("dp")
+    block = model_width // (seg_size * dp_size)
+    bounds = (0, 768, 1536, value_width)
+    pieces = []
+    for color, order in enumerate(ORDERS):
+        rows = jnp.asarray(row_order(order, seg_size, dp_size, block))
+        columns = value_grad[:, bounds[color] : bounds[color + 1]]
+        part = lax.dot_general(
+            scaled[:, rows], columns, (((0,), (0,)), ((), ())), preferred_element_type=jnp.float32
+        )
+        if color == len(ORDERS) - 1:
+            gain_block = jnp.zeros((model_width, 128), jnp.float32).at[:, 0].set(gain_grad[rows])
+            part = jnp.concatenate([part, gain_block], axis=1)
+        pieces.append(reduce_scatter_rows(part, order, where))
+    both = jnp.concatenate(pieces, axis=1)
     weight_part, gain_part = both[:, :value_width], both[:, value_width]
     return (hidden_grad.astype(jnp.bfloat16), summary_grad, weight_part, gain_part)
 

time: 719 us -> 602 us (0.84); the launches traced: 718 us -> 592 us
  waiting for transfers between devices: 574 us -> 220 us
  local copies, waits for them, and re-layouts: 15.6 us -> 152 us
  starting transfers between devices: 19.5 us -> 101 us
  other arithmetic: 39.3 us -> 55 us
  between operations: 14.2 us -> 1.83 us
    reduce_scatter x1 -> x0, waiting for transfers between devices: 382 us -> none  [local(): both = lax.psum_scatter(both, 'seg', scatter_dimension=0, tiled=True)]
    ppermute x0 -> x57, waiting for transfers between devices: none -> 102 us  [the longest x27 55 us: ring_reduce(): acc_a = lax.ppermute(acc_a, axes, forward) + own(ahead, coord - step)]
    ppermute x0 -> x57, starting transfers between devices: none -> 81.9 us  [the longest x27 59.1 us: ring_reduce(): acc_b = lax.ppermute(acc_b, axes, backward) + own(behind, coord + step)]
    gather x0 -> x4, local copies, waits for them, and re-layouts: none -> 74.9 us  [the longest x3 51.8 us: local(): scaled[:, rows]]
    unnamed x3 -> x0, waiting for transfers between devices: 73.8 us -> none
    dynamic_slice x0 -> x13, local copies, waits for them, and re-layouts: none -> 32.9 us  [the longest x10 20.8 us: own(): return lax.dynamic_index_in_dim(block, index % 4, 0, keepdims=False)]
    add x0 -> x57, other arithmetic: none -> 28.1 us  [the longest x3 17.6 us: reduce_scatter_rows(): part = keep + lax.ppermute(send, 'seg', shifted(seg_size, lambda i: i ^ 1))]
    concatenate x1 -> x8, other arithmetic: 23.4 us -> 6.2 us  [the longest x1 5.1 us: local(): part = jnp.concatenate([part, gain_block], axis=1)]
  transfers between devices with their start and end apart: 17 -> 72, of which waited for: 17 -> 40; matrix products, arithmetic and copies ran while one was open for 1% -> 22% of each run, Pallas kernels for 0% -> 0%
where the time goes in v2:
time: 602 us; the launch traced here: 592 us
  waiting for transfers between devices  220 us (37%)
  local copies, waits for them, and re-layouts  152 us (25%)
  starting transfers between devices  101 us (17%)
  matrix products  61.3 us (10%)
  other arithmetic  55 us (9%)
    ppermute x15, waiting for transfers between devices, passed_along(): return lax.ppermute(block, axis, route)  118 us
    ppermute x27, starting transfers between devices, ring_reduce(): acc_b = lax.ppermute(acc_b, axes, backward) + own(behind, coord + step)  59.1 us
    ppermute x27, waiting for transfers between devices, ring_reduce(): acc_a = lax.ppermute(acc_a, axes, forward) + own(ahead, coord - step)  55 us
    gather x3, local copies, waits for them, and re-layouts, local(): scaled[:, rows]  51.8 us
    ppermute x27, waiting for transfers between devices, ring_reduce(): acc_b = lax.ppermute(acc_b, axes, backward) + own(behind, coord + step)  47.5 us
    gather x1, local copies, waits for them, and re-layouts, local(): gain_grad[rows]  23 us
    dynamic_slice x10, local copies, waits for them, and re-layouts, own(): return lax.dynamic_index_in_dim(block, index % 4, 0, keepdims=False)  20.8 us
    ppermute x15, starting transfers between devices, passed_along(): return lax.ppermute(block, axis, route)  19.4 us
  transfers between devices with their start and end apart: 72, of which 40 were waited for; matrix products, arithmetic and copies ran while one was open for 22% of the time, Pallas kernels for 0%

profile of v2, /device:TPU:0, one launch (start us, length us, event | category | flops | bytes accessed | tf_op | source)
XLA Modules:
  0.0 592.5 jit_solution(11177460889411428155)
XLA Ops:
  9.1 4.5 fusion.50
  14.9 4.5 convolution_bitcast_fusion.1
  20.8 154.3 %while.11 = (s32[]{:T(128)}, f32[1,50,16,128]{3,2,0,1:T(8,128)S(1)}, f32[1,16,50,50]{3,2,1,0:T(8,128)S(1)}, f32[1,50,16,128]{3,1,2,0:T(8,128)S(1)}, s32[]{:T(128)}) while((s32[]{:T(128)}, f32[1,50,16,128]{3,2,0,1:T(8,128)S(1)}, f32[1,16,50,50]{3,2,1,0:T(8,128)S(1)}, f32[1,50,16,128]{3,1,2,0:T(8,128)S(1)}, s32[]{:T(128)}) %tuple.46), condition=%wide.region_4.5_spmd, body=%wide.region_3.4_spmd.sunk | while | flops 61542400 | bytes 3846501 | solution.py:136
  28.0 7.5 %collective-permute-done = f32[1,50,2048]{2,0,1:T(1,128)S(1)} collective-permute-done((f32[1,50,2048]{2,0,1:T(1,128)S(1)}, f32[1,50,2048]{2,0,1:T(1,128)S(1)}, u32[]{:S(2)}, u32[]{:S(2)}) %collective-permute-start) | collective-permute-done | bytes 409632 | tf_op jit(solution)/shard_map/while/body/eval_jaxpr/ppermute | solution.py:14
  37.9 8.0 %collective-permute-done = f32[1,50,2048]{2,0,1:T(1,128)S(1)} collective-permute-done((f32[1,50,2048]{2,0,1:T(1,128)S(1)}, f32[1,50,2048]{2,0,1:T(1,128)S(1)}, u32[]{:S(2)}, u32[]{:S(2)}) %collective-permute-start) | collective-permute-done | bytes 409632 | tf_op jit(solution)/shard_map/while/body/eval_jaxpr/ppermute | solution.py:14
  48.3 8.0 %collective-permute-done = f32[1,50,2048]{2,0,1:T(1,128)S(1)} collective-permute-done((f32[1,50,2048]{2,0,1:T(1,128)S(1)}, f32[1,50,2048]{2,0,1:T(1,128)S(1)}, u32[]{:S(2)}, u32[]{:S(2)}) %collective-permute-start) | collective-permute-done | bytes 409632 | tf_op jit(solution)/shard_map/while/body/eval_jaxpr/ppermute | solution.py:14
  58.7 8.0 %collective-permute-done = f32[1,50,2048]{2,0,1:T(1,128)S(1)} collective-permute-done((f32[1,50,2048]{2,0,1:T(1,128)S(1)}, f32[1,50,2048]{2,0,1:T(1,128)S(1)}, u32[]{:S(2)}, u32[]{:S(2)}) %collective-permute-start) | collective-permute-done | bytes 409632 | tf_op jit(solution)/shard_map/while/body/eval_jaxpr/ppermute | solution.py:14
  69.1 8.0 %collective-permute-done = f32[1,50,2048]{2,0,1:T(1,128)S(1)} collective-permute-done((f32[1,50,2048]{2,0,1:T(1,128)S(1)}, f32[1,50,2048]{2,0,1:T(1,128)S(1)}, u32[]{:S(2)}, u32[]{:S(2)}) %collective-permute-start) | collective-permute-done | bytes 409632 | tf_op jit(solution)/shard_map/while/body/eval_jaxpr/ppermute | solution.py:14
  79.4 8.0 %collective-permute-done = f32[1,50,2048]{2,0,1:T(1,128)S(1)} collective-permute-done((f32[1,50,2048]{2,0,1:T(1,128)S(1)}, f32[1,50,2048]{2,0,1:T(1,128)S(1)}, u32[]{:S(2)}, u32[]{:S(2)}) %collective-permute-start) | collective-permute-done | bytes 409632 | tf_op jit(solution)/shard_map/while/body/eval_jaxpr/ppermute | solution.py:14
  89.8 8.0 %collective-permute-done = f32[1,50,2048]{2,0,1:T(1,128)S(1)} collective-permute-done((f32[1,50,2048]{2,0,1:T(1,128)S(1)}, f32[1,50,2048]{2,0,1:T(1,128)S(1)}, u32[]{:S(2)}, u32[]{:S(2)}) %collective-permute-start) | collective-permute-done | bytes 409632 | tf_op jit(solution)/shard_map/while/body/eval_jaxpr/ppermute | solution.py:14
  100.2 8.0 %collective-permute-done = f32[1,50,2048]{2,0,1:T(1,128)S(1)} collective-permute-done((f32[1,50,2048]{2,0,1:T(1,128)S(1)}, f32[1,50,2048]{2,0,1:T(1,128)S(1)}, u32[]{:S(2)}, u32[]{:S(2)}) %collective-permute-start) | collective-permute-done | bytes 409632 | tf_op jit(solution)/shard_map/while/body/eval_jaxpr/ppermute | solution.py:14
  110.6 8.0 %collective-permute-done = f32[1,50,2048]{2,0,1:T(1,128)S(1)} collective-permute-done((f32[1,50,2048]{2,0,1:T(1,128)S(1)}, f32[1,50,2048]{2,0,1:T(1,128)S(1)}, u32[]{:S(2)}, u32[]{:S(2)}) %collective-permute-start) | collective-permute-done | bytes 409632 | tf_op jit(solution)/shard_map/while/body/eval_jaxpr/ppermute | solution.py:14
  121.0 8.8 %collective-permute-done = f32[1,50,2048]{2,0,1:T(1,128)S(1)} collective-permute-done((f32[1,50,2048]{2,0,1:T(1,128)S(1)}, f32[1,50,2048]{2,0,1:T(1,128)S(1)}, u32[]{:S(2)}, u32[]{:S(2)}) %collective-permute-start) | collective-permute-done | bytes 409632 | tf_op jit(solution)/shard_map/while/body/eval_jaxpr/ppermute | solution.py:14
  132.2 8.9 %collective-permute-done = f32[1,50,2048]{2,0,1:T(1,128)S(1)} collective-permute-done((f32[1,50,2048]{2,0,1:T(1,128)S(1)}, f32[1,50,2048]{2,0,1:T(1,128)S(1)}, u32[]{:S(2)}, u32[]{:S(2)}) %collective-permute-start) | collective-permute-done | bytes 409632 | tf_op jit(solution)/shard_map/while/body/eval_jaxpr/ppermute | solution.py:14
  143.5 8.9 %collective-permute-done = f32[1,50,2048]{2,0,1:T(1,128)S(1)} collective-permute-done((f32[1,50,2048]{2,0,1:T(1,128)S(1)}, f32[1,50,2048]{2,0,1:T(1,128)S(1)}, u32[]{:S(2)}, u32[]{:S(2)}) %collective-permute-start) | collective-permute-done | bytes 409632 | tf_op jit(solution)/shard_map/while/body/eval_jaxpr/ppermute | solution.py:14
  154.8 8.9 %collective-permute-done = f32[1,50,2048]{2,0,1:T(1,128)S(1)} collective-permute-done((f32[1,50,2048]{2,0,1:T(1,128)S(1)}, f32[1,50,2048]{2,0,1:T(1,128)S(1)}, u32[]{:S(2)}, u32[]{:S(2)}) %collective-permute-start) | collective-permute-done | bytes 409632 | tf_op jit(solution)/shard_map/while/body/eval_jaxpr/ppermute | solution.py:14
  166.1 8.9 %collective-permute-done = f32[1,50,2048]{2,0,1:T(1,128)S(1)} collective-permute-done((f32[1,50,2048]{2,0,1:T(1,128)S(1)}, f32[1,50,2048]{2,0,1:T(1,128)S(1)}, u32[]{:S(2)}, u32[]{:S(2)}) %collective-permute-start) | collective-permute-done | bytes 409632 | tf_op jit(solution)/shard_map/while/body/eval_jaxpr/ppermute | solution.py:14
  175.1 4.3 fusion.20
  182.9 19.0 %fusion.40 = f32[320,4096]{1,0:T(8,128)} fusion(bf16[4096,2048]{1,0:T(8,128)(2,1)} %param.16, bf16[40,8,16,128]{3,2,1,0:T(8,128)(2,1)} %bitcast.254), kind=kOutput, calls=%fused_computation.162 | convolution fusion | flops 5368709120 | bytes 23330816 | tf_op jit(solution)/shard_map/dot_general | solution.py:148
  202.5 5.9 fusion.14
  208.4 3.3 copy.44
  211.7 23.0 %gather_fusion.3 = f32[4096]{0:T(1024)S(1)} fusion(f32[4096]{0:T(1024)S(1)} %get-tuple-element.47, s32[4096]{0:T(1024)S(1)} %broadcast_clamp_fusion), kind=kCustom, calls=%fused_computation.3 | custom fusion | bytes 49152 | tf_op jit(solution)/shard_map/gather | solution.py:178
  234.7 17.6 %gather_fusion.2 = bf16[4096,320]{1,0:T(8,128)(2,1)} fusion(bf16[320,4096]{0,1:T(8,128)(2,1)S(1)} %copy.44, s32[4096]{0:T(1024)S(1)} %broadcast_clamp_fusion), kind=kCustom, calls=%fused_computation.2 | custom fusion | bytes 5259264 | tf_op jit(solution)/shard_map/gather | solution.py:175
  253.0 4.3 fusion.31
  257.3 5.1 select_maximum_fusion
  262.4 5.5 constant_dynamic-slice_fusion.8
  267.9 7.0 %collective-permute-start.39 = (f32[2048,640]{0,1:T(8,128)}, f32[2048,640]{0,1:T(8,128)}, u32[]{:S(2)}, u32[]{:S(2)}) collective-permute-start(f32[2048,640]{0,1:T(8,128)} %constant_dynamic-slice_fusion.8), channel_id=1, source_target_pairs={{0,8},{8,0},{16,24},{24,16},{32,40},{40,32},{48,56},{56,48},{64,72... | collective-permute-start | bytes 15728648 | tf_op jit(solution)/shard_map/ppermute | solution.py:110
  274.9 17.1 %gather_fusion.1 = bf16[4096,320]{1,0:T(8,128)(2,1)} fusion(bf16[320,4096]{0,1:T(8,128)(2,1)S(1)} %copy.44, s32[4096]{0:T(1024)S(1)} %broadcast_clamp_fusion.1), kind=kCustom, calls=%fused_computation.1 | custom fusion | bytes 5259264 | tf_op jit(solution)/shard_map/gather | solution.py:175
  292.0 5.5 fusion.25
  297.5 3.3 constant_dynamic-slice_fusion.9
  300.8 3.1 copy-done.1
  304.0 17.1 %gather_fusion = bf16[4096,320]{1,0:T(8,128)(2,1)} fusion(bf16[320,4096]{0,1:T(8,128)(2,1)S(1)} %copy.44, s32[4096]{0:T(1024)S(1)} %broadcast_clamp_fusion.2), kind=kCustom, calls=%fused_computation | custom fusion | bytes 5259264 | tf_op jit(solution)/shard_map/gather | solution.py:175
  321.1 5.5 fusion.27
  326.6 3.3 constant_dynamic-slice_fusion.10
  329.9 3.2 copy-done
  333.6 7.9 %dynamic-slice_add_fusion.2 = f32[2048,640]{0,1:T(8,128)} fusion(f32[2048,640]{0,1:T(8,128)} %collective-permute-done.39, f32[4096,640]{0,1:T(8,128)} %select_maximum_fusion, s32[]{:T(128)S(6)} %select_n.371), kind=kLoop, calls=%fused_computation.30 | loop fusion | flops 1310720 | bytes 15728644 | tf_op jit(solution)/shard_map/add | solution.py:110
  341.4 8.3 %reshape.331 = f32[4,2,256,640]{2,1,0,3:T(2,128)} reshape(f32[2048,640]{0,1:T(8,128)} %dynamic-slice_add_fusion.2) | data formatting | bytes 10485760 | tf_op jit(solution)/shard_map/reshape | solution.py:45
  349.7 10.0 %fusion.43 = (f32[4,1,256,640]{2,1,0,3:T(1,128)}, f32[4,1,256,640]{2,1,0,3:T(1,128)S(1)}) fusion(f32[4,2,256,640]{2,1,0,3:T(2,128)} %reshape.331), kind=kLoop, calls=%fused_computation.165 | loop fusion | bytes 10485760 | tf_op jit(solution)/shard_map/slice | solution.py:46
  359.7 2.9 constant_dynamic-slice_fusion
  364.1 4.0 collective-permute-start.43
  368.2 4.9 constant_dynamic-slice_fusion.4
  375.3 5.5 fusion.12
  395.1 3.2 collective-permute-start.44
  400.3 5.6 dynamic-slice_add_fusion
  407.6 11.0 %collective-permute-start.24 = (f32[256,768]{1,0:T(8,128)}, f32[256,768]{1,0:T(8,128)}, u32[]{:S(2)}, u32[]{:S(2)}) collective-permute-start(f32[256,768]{1,0:T(8,128)} %dynamic-slice_bitcast_fusion), channel_id=1, source_target_pairs={{0,20},{1,21},{2,22},{3,23},{4,16},{5,17},{6,18},{7,19},{8,28},{9,... | collective-permute-start | bytes 2359304 | tf_op jit(solution)/shard_map/ppermute | solution.py:55
  419.6 4.1 dynamic-slice_add_fusion.1
  427.9 3.3 collective-permute-start.45
  436.3 3.1 collective-permute-done.21
  446.6 4.6 collective-permute-done.42
  453.8 11.7 %collective-permute-done.49 = f32[64,640]{1,0:T(8,128)S(1)} collective-permute-done((f32[64,640]{1,0:T(8,128)S(1)}, f32[64,640]{1,0:T(8,128)S(1)}, u32[]{:S(2)}, u32[]{:S(2)}) %collective-permute-start.49) | collective-permute-done | bytes 163872 | tf_op jit(solution)/shard_map/ppermute | solution.py:55
  467.0 8.4 %collective-permute-done.46 = f32[64,640]{1,0:T(8,128)S(1)} collective-permute-done((f32[64,640]{1,0:T(8,128)S(1)}, f32[64,640]{1,0:T(8,128)S(1)}, u32[]{:S(2)}, u32[]{:S(2)}) %collective-permute-start.46) | collective-permute-done | bytes 163872 | tf_op jit(solution)/shard_map/ppermute | solution.py:54
  475.4 5.3 collective-permute-done.50
  480.8 6.5 %collective-permute-done.47 = f32[64,640]{1,0:T(8,128)S(1)} collective-permute-done((f32[64,640]{1,0:T(8,128)S(1)}, f32[64,640]{1,0:T(8,128)S(1)}, u32[]{:S(2)}, u32[]{:S(2)}) %collective-permute-start.47) | collective-permute-done | bytes 163872 | tf_op jit(solution)/shard_map/ppermute | solution.py:54
  487.3 5.3 collective-permute-done.51
  492.6 6.5 %collective-permute-done.48 = f32[64,640]{1,0:T(8,128)S(1)} collective-permute-done((f32[64,640]{1,0:T(8,128)S(1)}, f32[64,640]{1,0:T(8,128)S(1)}, u32[]{:S(2)}, u32[]{:S(2)}) %collective-permute-start.48) | collective-permute-done | bytes 163872 | tf_op jit(solution)/shard_map/ppermute | solution.py:54
  505.0 3.6 collective-permute-done.52
  513.1 4.8 collective-permute-done.53
  522.3 5.8 collective-permute-done.54
  533.5 11.6 %collective-permute-done.26 = f32[256,768]{1,0:T(8,128)S(1)} collective-permute-done((f32[256,768]{1,0:T(8,128)S(1)}, f32[256,768]{1,0:T(8,128)S(1)}, u32[]{:S(2)}, u32[]{:S(2)}) %collective-permute-start.26) | collective-permute-done | bytes 786464 | tf_op jit(solution)/shard_map/ppermute | solution.py:55
  545.2 2.9 collective-permute-done.23
  566.5 3.6 collective-permute-done.29
  574.5 3.1 collective-permute-start.37
  580.0 3.3 collective-permute-start.38
  588.7 2.9 collective-permute-done.16
  (316 shorter events, 148.9 us)
Async XLA Ops:
  26.7 8.8 %collective-permute-start = (f32[1,50,2048]{2,0,1:T(1,128)S(1)}, f32[1,50,2048]{2,0,1:T(1,128)S(1)}, u32[]{:S(2)}, u32[]{:S(2)}) collective-permute-start(f32[1,50,2048]{2,0,1:T(1,128)S(1)} %bitcast.248), channel_id=1, source_target_pairs={{8,0},{16,8},{24,16},{32,24},{40,32},{48,40},{56,48},{64,56},{72,6... | collective-permute-start | bytes 1228808 | tf_op jit(solution)/shard_map/while/body/eval_jaxpr/ppermute | solution.py:14
  36.6 9.3 %collective-permute-start = (f32[1,50,2048]{2,0,1:T(1,128)S(1)}, f32[1,50,2048]{2,0,1:T(1,128)S(1)}, u32[]{:S(2)}, u32[]{:S(2)}) collective-permute-start(f32[1,50,2048]{2,0,1:T(1,128)S(1)} %bitcast.248), channel_id=1, source_target_pairs={{8,0},{16,8},{24,16},{32,24},{40,32},{48,40},{56,48},{64,56},{72,6... | collective-permute-start | bytes 1228808 | tf_op jit(solution)/shard_map/while/body/eval_jaxpr/ppermute | solution.py:14
  47.0 9.3 %collective-permute-start = (f32[1,50,2048]{2,0,1:T(1,128)S(1)}, f32[1,50,2048]{2,0,1:T(1,128)S(1)}, u32[]{:S(2)}, u32[]{:S(2)}) collective-permute-start(f32[1,50,2048]{2,0,1:T(1,128)S(1)} %bitcast.248), channel_id=1, source_target_pairs={{8,0},{16,8},{24,16},{32,24},{40,32},{48,40},{56,48},{64,56},{72,6... | collective-permute-start | bytes 1228808 | tf_op jit(solution)/shard_map/while/body/eval_jaxpr/ppermute | solution.py:14
  57.4 9.3 %collective-permute-start = (f32[1,50,2048]{2,0,1:T(1,128)S(1)}, f32[1,50,2048]{2,0,1:T(1,128)S(1)}, u32[]{:S(2)}, u32[]{:S(2)}) collective-permute-start(f32[1,50,2048]{2,0,1:T(1,128)S(1)} %bitcast.248), channel_id=1, source_target_pairs={{8,0},{16,8},{24,16},{32,24},{40,32},{48,40},{56,48},{64,56},{72,6... | collective-permute-start | bytes 1228808 | tf_op jit(solution)/shard_map/while/body/eval_jaxpr/ppermute | solution.py:14
  67.8 9.3 %collective-permute-start = (f32[1,50,2048]{2,0,1:T(1,128)S(1)}, f32[1,50,2048]{2,0,1:T(1,128)S(1)}, u32[]{:S(2)}, u32[]{:S(2)}) collective-permute-start(f32[1,50,2048]{2,0,1:T(1,128)S(1)} %bitcast.248), channel_id=1, source_target_pairs={{8,0},{16,8},{24,16},{32,24},{40,32},{48,40},{56,48},{64,56},{72,6... | collective-permute-start | bytes 1228808 | tf_op jit(solution)/shard_map/while/body/eval_jaxpr/ppermute | solution.py:14
  78.1 9.3 %collective-permute-start = (f32[1,50,2048]{2,0,1:T(1,128)S(1)}, f32[1,50,2048]{2,0,1:T(1,128)S(1)}, u32[]{:S(2)}, u32[]{:S(2)}) collective-permute-start(f32[1,50,2048]{2,0,1:T(1,128)S(1)} %bitcast.248), channel_id=1, source_target_pairs={{8,0},{16,8},{24,16},{32,24},{40,32},{48,40},{56,48},{64,56},{72,6... | collective-permute-start | bytes 1228808 | tf_op jit(solution)/shard_map/while/body/eval_jaxpr/ppermute | solution.py:14
  88.5 9.3 %collective-permute-start = (f32[1,50,2048]{2,0,1:T(1,128)S(1)}, f32[1,50,2048]{2,0,1:T(1,128)S(1)}, u32[]{:S(2)}, u32[]{:S(2)}) collective-permute-start(f32[1,50,2048]{2,0,1:T(1,128)S(1)} %bitcast.248), channel_id=1, source_target_pairs={{8,0},{16,8},{24,16},{32,24},{40,32},{48,40},{56,48},{64,56},{72,6... | collective-permute-start | bytes 1228808 | tf_op jit(solution)/shard_map/while/body/eval_jaxpr/ppermute | solution.py:14
  98.9 9.3 %collective-permute-start = (f32[1,50,2048]{2,0,1:T(1,128)S(1)}, f32[1,50,2048]{2,0,1:T(1,128)S(1)}, u32[]{:S(2)}, u32[]{:S(2)}) collective-permute-start(f32[1,50,2048]{2,0,1:T(1,128)S(1)} %bitcast.248), channel_id=1, source_target_pairs={{8,0},{16,8},{24,16},{32,24},{40,32},{48,40},{56,48},{64,56},{72,6... | collective-permute-start | bytes 1228808 | tf_op jit(solution)/shard_map/while/body/eval_jaxpr/ppermute | solution.py:14
  109.3 9.3 %collective-permute-start = (f32[1,50,2048]{2,0,1:T(1,128)S(1)}, f32[1,50,2048]{2,0,1:T(1,128)S(1)}, u32[]{:S(2)}, u32[]{:S(2)}) collective-permute-start(f32[1,50,2048]{2,0,1:T(1,128)S(1)} %bitcast.248), channel_id=1, source_target_pairs={{8,0},{16,8},{24,16},{32,24},{40,32},{48,40},{56,48},{64,56},{72,6... | collective-permute-start | bytes 1228808 | tf_op jit(solution)/shard_map/while/body/eval_jaxpr/ppermute | solution.py:14
  119.7 10.2 %collective-permute-start = (f32[1,50,2048]{2,0,1:T(1,128)S(1)}, f32[1,50,2048]{2,0,1:T(1,128)S(1)}, u32[]{:S(2)}, u32[]{:S(2)}) collective-permute-start(f32[1,50,2048]{2,0,1:T(1,128)S(1)} %bitcast.248), channel_id=1, source_target_pairs={{8,0},{16,8},{24,16},{32,24},{40,32},{48,40},{56,48},{64,56},{72,6... | collective-permute-start | bytes 1228808 | tf_op jit(solution)/shard_map/while/body/eval_jaxpr/ppermute | solution.py:14
  130.9 10.2 %collective-permute-start = (f32[1,50,2048]{2,0,1:T(1,128)S(1)}, f32[1,50,2048]{2,0,1:T(1,128)S(1)}, u32[]{:S(2)}, u32[]{:S(2)}) collective-permute-start(f32[1,50,2048]{2,0,1:T(1,128)S(1)} %bitcast.248), channel_id=1, source_target_pairs={{8,0},{16,8},{24,16},{32,24},{40,32},{48,40},{56,48},{64,56},{72,6... | collective-permute-start | bytes 1228808 | tf_op jit(solution)/shard_map/while/body/eval_jaxpr/ppermute | solution.py:14
  142.2 10.2 %collective-permute-start = (f32[1,50,2048]{2,0,1:T(1,128)S(1)}, f32[1,50,2048]{2,0,1:T(1,128)S(1)}, u32[]{:S(2)}, u32[]{:S(2)}) collective-permute-start(f32[1,50,2048]{2,0,1:T(1,128)S(1)} %bitcast.248), channel_id=1, source_target_pairs={{8,0},{16,8},{24,16},{32,24},{40,32},{48,40},{56,48},{64,56},{72,6... | collective-permute-start | bytes 1228808 | tf_op jit(solution)/shard_map/while/body/eval_jaxpr/ppermute | solution.py:14
  153.5 10.2 %collective-permute-start = (f32[1,50,2048]{2,0,1:T(1,128)S(1)}, f32[1,50,2048]{2,0,1:T(1,128)S(1)}, u32[]{:S(2)}, u32[]{:S(2)}) collective-permute-start(f32[1,50,2048]{2,0,1:T(1,128)S(1)} %bitcast.248), channel_id=1, source_target_pairs={{8,0},{16,8},{24,16},{32,24},{40,32},{48,40},{56,48},{64,56},{72,6... | collective-permute-start | bytes 1228808 | tf_op jit(solution)/shard_map/while/body/eval_jaxpr/ppermute | solution.py:14
  164.8 10.2 %collective-permute-start = (f32[1,50,2048]{2,0,1:T(1,128)S(1)}, f32[1,50,2048]{2,0,1:T(1,128)S(1)}, u32[]{:S(2)}, u32[]{:S(2)}) collective-permute-start(f32[1,50,2048]{2,0,1:T(1,128)S(1)} %bitcast.248), channel_id=1, source_target_pairs={{8,0},{16,8},{24,16},{32,24},{40,32},{48,40},{56,48},{64,56},{72,6... | collective-permute-start | bytes 1228808 | tf_op jit(solution)/shard_map/while/body/eval_jaxpr/ppermute | solution.py:14
  267.9 65.7 %collective-permute-start.39 = (f32[2048,640]{0,1:T(8,128)}, f32[2048,640]{0,1:T(8,128)}, u32[]{:S(2)}, u32[]{:S(2)}) collective-permute-start(f32[2048,640]{0,1:T(8,128)} %constant_dynamic-slice_fusion.8), channel_id=1, source_target_pairs={{0,8},{8,0},{16,24},{24,16},{32,40},{40,32},{48,56},{56,48},{64,72... | collective-permute-start | bytes 15728648 | tf_op jit(solution)/shard_map/ppermute | solution.py:110
  304.0 96.4 %collective-permute-start.20 = (f32[2048,768]{1,0:T(8,128)}, f32[2048,768]{1,0:T(8,128)}, u32[]{:S(2)}, u32[]{:S(2)}) collective-permute-start(f32[2048,768]{1,0:T(8,128)} %constant_dynamic-slice_fusion.9), channel_id=1, source_target_pairs={{0,8},{8,0},{16,24},{24,16},{32,40},{40,32},{48,56},{56,48},{64,72... | collective-permute-start | bytes 18874376 | tf_op jit(solution)/shard_map/ppermute | solution.py:110
  333.1 86.5 %collective-permute-start.1 = (f32[2048,768]{1,0:T(8,128)}, f32[2048,768]{1,0:T(8,128)}, u32[]{:S(2)}, u32[]{:S(2)}) collective-permute-start(f32[2048,768]{1,0:T(8,128)} %constant_dynamic-slice_fusion.10), channel_id=1, source_target_pairs={{0,8},{8,0},{16,24},{24,16},{32,40},{40,32},{48,56},{56,48},{64,72... | collective-permute-start | bytes 18874376 | tf_op jit(solution)/shard_map/ppermute | solution.py:110
  364.1 28.9 %collective-permute-start.43 = (f32[256,640]{1,0:T(8,128)}, f32[256,640]{1,0:T(8,128)}, u32[]{:S(2)}, u32[]{:S(2)}) collective-permute-start(f32[256,640]{1,0:T(8,128)} %bitcast.85), channel_id=1, source_target_pairs={{0,3},{1,0},{2,1},{3,2},{4,7},{5,4},{6,5},{7,6},{8,11},{9,8},{10,9... | collective-permute-start | bytes 1966088 | tf_op jit(solution)/shard_map/ppermute | solution.py:55
  375.1 23.2 %collective-permute-start.40 = (f32[256,640]{1,0:T(8,128)}, f32[256,640]{1,0:T(8,128)}, u32[]{:S(2)}, u32[]{:S(2)}) collective-permute-start(f32[256,640]{1,0:T(8,128)} %bitcast.265), channel_id=1, source_target_pairs={{0,1},{1,2},{2,3},{3,0},{4,5},{5,6},{6,7},{7,4},{8,9},{9,10},{10,1... | collective-permute-start | bytes 1966088 | tf_op jit(solution)/shard_map/ppermute | solution.py:54
  395.1 30.3 %collective-permute-start.44 = (f32[256,640]{1,0:T(8,128)}, f32[256,640]{1,0:T(8,128)}, u32[]{:S(2)}, u32[]{:S(2)}) collective-permute-start(f32[256,640]{1,0:T(8,128)} %bitcast_add_fusion.14), channel_id=1, source_target_pairs={{0,3},{1,0},{2,1},{3,2},{4,7},{5,4},{6,5},{7,6},{8,11},{9,8},{10,9... | collective-permute-start | bytes 1966088 | tf_op jit(solution)/shard_map/ppermute | solution.py:55
  400.3 27.6 %collective-permute-start.41 = (f32[256,640]{1,0:T(8,128)}, f32[256,640]{1,0:T(8,128)}, u32[]{:S(2)}, u32[]{:S(2)}) collective-permute-start(f32[256,640]{1,0:T(8,128)} %bitcast_add_fusion.17), channel_id=1, source_target_pairs={{0,1},{1,2},{2,3},{3,0},{4,5},{5,6},{6,7},{7,4},{8,9},{9,10},{10,1... | collective-permute-start | bytes 1966088 | tf_op jit(solution)/shard_map/ppermute | solution.py:54
  407.6 27.5 %collective-permute-start.24 = (f32[256,768]{1,0:T(8,128)}, f32[256,768]{1,0:T(8,128)}, u32[]{:S(2)}, u32[]{:S(2)}) collective-permute-start(f32[256,768]{1,0:T(8,128)} %dynamic-slice_bitcast_fusion), channel_id=1, source_target_pairs={{0,20},{1,21},{2,22},{3,23},{4,16},{5,17},{6,18},{7,19},{8,28},{9,... | collective-permute-start | bytes 2359304 | tf_op jit(solution)/shard_map/ppermute | solution.py:55
  419.5 19.9 %collective-permute-start.21 = (f32[256,768]{1,0:T(8,128)}, f32[256,768]{1,0:T(8,128)}, u32[]{:S(2)}, u32[]{:S(2)}) collective-permute-start(f32[256,768]{1,0:T(8,128)} %dynamic-slice_bitcast_fusion.1), channel_id=1, source_target_pairs={{0,16},{1,17},{2,18},{3,19},{4,20},{5,21},{6,22},{7,23},{8,24},{9,... | collective-permute-start | bytes 2359304 | tf_op jit(solution)/shard_map/ppermute | solution.py:54
  424.5 18.5 %collective-permute-start.5 = (f32[256,768]{1,0:T(8,128)S(1)}, f32[256,768]{1,0:T(8,128)S(1)}, u32[]{:S(2)}, u32[]{:S(2)}) collective-permute-start(f32[256,768]{1,0:T(8,128)S(1)} %dynamic-slice_bitcast_fusion.2), channel_id=1, source_target_pairs={{0,96},{8,104},{16,112},{24,120},{32,0},{40,8},{48,16},{56,24},{64... | collective-permute-start | bytes 2359304 | tf_op jit(solution)/shard_map/ppermute | solution.py:55
  425.4 28.0 %collective-permute-start.2 = (f32[256,768]{1,0:T(8,128)S(1)}, f32[256,768]{1,0:T(8,128)S(1)}, u32[]{:S(2)}, u32[]{:S(2)}) collective-permute-start(f32[256,768]{1,0:T(8,128)S(1)} %dynamic-slice_bitcast_fusion.3), channel_id=1, source_target_pairs={{0,32},{8,40},{16,48},{24,56},{32,64},{40,72},{48,80},{56,88},{64,... | collective-permute-start | bytes 2359304 | tf_op jit(solution)/shard_map/ppermute | solution.py:54
  427.9 16.3 %collective-permute-start.45 = (f32[256,640]{1,0:T(8,128)S(1)}, f32[256,640]{1,0:T(8,128)S(1)}, u32[]{:S(2)}, u32[]{:S(2)}) collective-permute-start(f32[256,640]{1,0:T(8,128)S(1)} %bitcast_add_fusion.13), channel_id=1, source_target_pairs={{0,3},{1,0},{2,1},{3,2},{4,7},{5,4},{6,5},{7,6},{8,11},{9,8},{10,9... | collective-permute-start | bytes 1966088 | tf_op jit(solution)/shard_map/ppermute | solution.py:55
  435.1 16.1 %collective-permute-start.42 = (f32[256,640]{1,0:T(8,128)S(1)}, f32[256,640]{1,0:T(8,128)S(1)}, u32[]{:S(2)}, u32[]{:S(2)}) collective-permute-start(f32[256,640]{1,0:T(8,128)S(1)} %bitcast_add_fusion.16), channel_id=1, source_target_pairs={{0,1},{1,2},{2,3},{3,0},{4,5},{5,6},{6,7},{7,4},{8,9},{9,10},{10,1... | collective-permute-start | bytes 1966088 | tf_op jit(solution)/shard_map/ppermute | solution.py:54
  439.4 89.3 %collective-permute-start.25 = (f32[256,768]{1,0:T(8,128)S(1)}, f32[256,768]{1,0:T(8,128)S(1)}, u32[]{:S(2)}, u32[]{:S(2)}) collective-permute-start(f32[256,768]{1,0:T(8,128)S(1)} %bitcast_add_fusion.2), channel_id=1, source_target_pairs={{0,20},{1,21},{2,22},{3,23},{4,16},{5,17},{6,18},{7,19},{8,28},{9,... | collective-permute-start | bytes 2359304 | tf_op jit(solution)/shard_map/ppermute | solution.py:55
  442.9 87.9 %collective-permute-start.22 = (f32[256,768]{1,0:T(8,128)S(1)}, f32[256,768]{1,0:T(8,128)S(1)}, u32[]{:S(2)}, u32[]{:S(2)}) collective-permute-start(f32[256,768]{1,0:T(8,128)S(1)} %bitcast_add_fusion.5), channel_id=1, source_target_pairs={{0,16},{1,17},{2,18},{3,19},{4,20},{5,21},{6,22},{7,23},{8,24},{9,... | collective-permute-start | bytes 2359304 | tf_op jit(solution)/shard_map/ppermute | solution.py:54
  444.2 87.0 %collective-permute-start.6 = (f32[256,768]{1,0:T(8,128)S(1)}, f32[256,768]{1,0:T(8,128)S(1)}, u32[]{:S(2)}, u32[]{:S(2)}) collective-permute-start(f32[256,768]{1,0:T(8,128)S(1)} %bitcast_add_fusion.8), channel_id=1, source_target_pairs={{0,96},{8,104},{16,112},{24,120},{32,0},{40,8},{48,16},{56,24},{64... | collective-permute-start | bytes 2359304 | tf_op jit(solution)/shard_map/ppermute | solution.py:55
  451.5 14.0 %collective-permute-start.49 = (f32[64,640]{1,0:T(8,128)S(1)}, f32[64,640]{1,0:T(8,128)S(1)}, u32[]{:S(2)}, u32[]{:S(2)}) collective-permute-start(f32[64,640]{1,0:T(8,128)S(1)} %dynamic-slice_bitcast_fusion.8), channel_id=1, source_target_pairs={{0,96},{8,104},{16,112},{24,120},{32,0},{40,8},{48,16},{56,24},{64... | collective-permute-start | bytes 491528 | tf_op jit(solution)/shard_map/ppermute | solution.py:55
  453.6 79.3 %collective-permute-start.3 = (f32[256,768]{1,0:T(8,128)S(1)}, f32[256,768]{1,0:T(8,128)S(1)}, u32[]{:S(2)}, u32[]{:S(2)}) collective-permute-start(f32[256,768]{1,0:T(8,128)S(1)} %bitcast_add_fusion.11), channel_id=1, source_target_pairs={{0,32},{8,40},{16,48},{24,56},{32,64},{40,72},{48,80},{56,88},{64,... | collective-permute-start | bytes 2359304 | tf_op jit(solution)/shard_map/ppermute | solution.py:54
  465.5 9.9 %collective-permute-start.46 = (f32[64,640]{1,0:T(8,128)S(1)}, f32[64,640]{1,0:T(8,128)S(1)}, u32[]{:S(2)}, u32[]{:S(2)}) collective-permute-start(f32[64,640]{1,0:T(8,128)S(1)} %dynamic-slice_bitcast_fusion.9), channel_id=1, source_target_pairs={{0,32},{8,40},{16,48},{24,56},{32,64},{40,72},{48,80},{56,88},{64,... | collective-permute-start | bytes 491528 | tf_op jit(solution)/shard_map/ppermute | solution.py:54
  475.4 5.3 collective-permute-start.50
  480.7 6.5 %collective-permute-start.47 = (f32[64,640]{1,0:T(8,128)S(1)}, f32[64,640]{1,0:T(8,128)S(1)}, u32[]{:S(2)}, u32[]{:S(2)}) collective-permute-start(f32[64,640]{1,0:T(8,128)S(1)} %bitcast_add_fusion.35), channel_id=1, source_target_pairs={{0,32},{8,40},{16,48},{24,56},{32,64},{40,72},{48,80},{56,88},{64,... | collective-permute-start | bytes 491528 | tf_op jit(solution)/shard_map/ppermute | solution.py:54
  487.3 5.3 collective-permute-start.51
  492.6 6.5 %collective-permute-start.48 = (f32[64,640]{1,0:T(8,128)S(1)}, f32[64,640]{1,0:T(8,128)S(1)}, u32[]{:S(2)}, u32[]{:S(2)}) collective-permute-start(f32[64,640]{1,0:T(8,128)S(1)} %bitcast_add_fusion.34), channel_id=1, source_target_pairs={{0,32},{8,40},{16,48},{24,56},{32,64},{40,72},{48,80},{56,88},{64,... | collective-permute-start | bytes 491528 | tf_op jit(solution)/shard_map/ppermute | solution.py:54
  503.3 5.3 collective-permute-start.52
  522.3 5.8 collective-permute-start.54
  528.9 16.3 %collective-permute-start.26 = (f32[256,768]{1,0:T(8,128)S(1)}, f32[256,768]{1,0:T(8,128)S(1)}, u32[]{:S(2)}, u32[]{:S(2)}) collective-permute-start(f32[256,768]{1,0:T(8,128)S(1)} %bitcast_add_fusion.1), channel_id=1, source_target_pairs={{0,20},{1,21},{2,22},{3,23},{4,16},{5,17},{6,18},{7,19},{8,28},{9,... | collective-permute-start | bytes 2359304 | tf_op jit(solution)/shard_map/ppermute | solution.py:55
  530.9 17.2 %collective-permute-start.23 = (f32[256,768]{1,0:T(8,128)S(1)}, f32[256,768]{1,0:T(8,128)S(1)}, u32[]{:S(2)}, u32[]{:S(2)}) collective-permute-start(f32[256,768]{1,0:T(8,128)S(1)} %bitcast_add_fusion.4), channel_id=1, source_target_pairs={{0,16},{1,17},{2,18},{3,19},{4,20},{5,21},{6,22},{7,23},{8,24},{9,... | collective-permute-start | bytes 2359304 | tf_op jit(solution)/shard_map/ppermute | solution.py:54
  531.2 19.4 %collective-permute-start.7 = (f32[256,768]{1,0:T(8,128)S(1)}, f32[256,768]{1,0:T(8,128)S(1)}, u32[]{:S(2)}, u32[]{:S(2)}) collective-permute-start(f32[256,768]{1,0:T(8,128)S(1)} %bitcast_add_fusion.7), channel_id=1, source_target_pairs={{0,96},{8,104},{16,112},{24,120},{32,0},{40,8},{48,16},{56,24},{64... | collective-permute-start | bytes 2359304 | tf_op jit(solution)/shard_map/ppermute | solution.py:55
  533.0 17.8 %collective-permute-start.4 = (f32[256,768]{1,0:T(8,128)S(1)}, f32[256,768]{1,0:T(8,128)S(1)}, u32[]{:S(2)}, u32[]{:S(2)}) collective-permute-start(f32[256,768]{1,0:T(8,128)S(1)} %bitcast_add_fusion.10), channel_id=1, source_target_pairs={{0,32},{8,40},{16,48},{24,56},{32,64},{40,72},{48,80},{56,88},{64,... | collective-permute-start | bytes 2359304 | tf_op jit(solution)/shard_map/ppermute | solution.py:54
  548.5 5.7 collective-permute-start.30
  548.6 7.0 %collective-permute-start.27 = (f32[64,768]{1,0:T(8,128)S(1)}, f32[64,768]{1,0:T(8,128)S(1)}, u32[]{:S(2)}, u32[]{:S(2)}) collective-permute-start(f32[64,768]{1,0:T(8,128)S(1)} %dynamic-slice_bitcast_fusion.5), channel_id=1, source_target_pairs={{0,1},{1,2},{2,3},{3,0},{4,5},{5,6},{6,7},{7,4},{8,9},{9,10},{10,1... | collective-permute-start | bytes 589832 | tf_op jit(solution)/shard_map/ppermute | solution.py:54
  551.2 5.7 collective-permute-start.11
  551.3 6.9 %collective-permute-start.8 = (f32[64,768]{1,0:T(8,128)S(1)}, f32[64,768]{1,0:T(8,128)S(1)}, u32[]{:S(2)}, u32[]{:S(2)}) collective-permute-start(f32[64,768]{1,0:T(8,128)S(1)} %dynamic-slice_bitcast_fusion.7), channel_id=1, source_target_pairs={{0,16},{1,17},{2,18},{3,19},{4,20},{5,21},{6,22},{7,23},{8,24},{9,... | collective-permute-start | bytes 589832 | tf_op jit(solution)/shard_map/ppermute | solution.py:54
  554.3 5.7 collective-permute-start.31
  555.6 7.1 %collective-permute-start.28 = (f32[64,768]{1,0:T(8,128)S(1)}, f32[64,768]{1,0:T(8,128)S(1)}, u32[]{:S(2)}, u32[]{:S(2)}) collective-permute-start(f32[64,768]{1,0:T(8,128)S(1)} %bitcast_add_fusion.23), channel_id=1, source_target_pairs={{0,1},{1,2},{2,3},{3,0},{4,5},{5,6},{6,7},{7,4},{8,9},{9,10},{10,1... | collective-permute-start | bytes 589832 | tf_op jit(solution)/shard_map/ppermute | solution.py:54
  556.9 5.9 collective-permute-start.12
  558.2 6.9 %collective-permute-start.9 = (f32[64,768]{1,0:T(8,128)S(1)}, f32[64,768]{1,0:T(8,128)S(1)}, u32[]{:S(2)}, u32[]{:S(2)}) collective-permute-start(f32[64,768]{1,0:T(8,128)S(1)} %bitcast_add_fusion.29), channel_id=1, source_target_pairs={{0,16},{1,17},{2,18},{3,19},{4,20},{5,21},{6,22},{7,23},{8,24},{9,... | collective-permute-start | bytes 589832 | tf_op jit(solution)/shard_map/ppermute | solution.py:54
  560.0 6.4 %collective-permute-start.32 = (f32[64,768]{1,0:T(8,128)S(1)}, f32[64,768]{1,0:T(8,128)S(1)}, u32[]{:S(2)}, u32[]{:S(2)}) collective-permute-start(f32[64,768]{1,0:T(8,128)S(1)} %bitcast_add_fusion.19), channel_id=1, source_target_pairs={{0,3},{1,0},{2,1},{3,2},{4,7},{5,4},{6,5},{7,6},{8,11},{9,8},{10,9... | collective-permute-start | bytes 589832 | tf_op jit(solution)/shard_map/ppermute | solution.py:55
  562.7 7.3 %collective-permute-start.29 = (f32[64,768]{1,0:T(8,128)S(1)}, f32[64,768]{1,0:T(8,128)S(1)}, u32[]{:S(2)}, u32[]{:S(2)}) collective-permute-start(f32[64,768]{1,0:T(8,128)S(1)} %bitcast_add_fusion.22), channel_id=1, source_target_pairs={{0,1},{1,2},{2,3},{3,0},{4,5},{5,6},{6,7},{7,4},{8,9},{9,10},{10,1... | collective-permute-start | bytes 589832 | tf_op jit(solution)/shard_map/ppermute | solution.py:54
  562.8 9.4 %collective-permute-start.13 = (f32[64,768]{1,0:T(8,128)S(1)}, f32[64,768]{1,0:T(8,128)S(1)}, u32[]{:S(2)}, u32[]{:S(2)}) collective-permute-start(f32[64,768]{1,0:T(8,128)S(1)} %bitcast_add_fusion.25), channel_id=1, source_target_pairs={{0,20},{1,21},{2,22},{3,23},{4,16},{5,17},{6,18},{7,19},{8,28},{9,... | collective-permute-start | bytes 589832 | tf_op jit(solution)/shard_map/ppermute | solution.py:55
  565.2 7.1 %collective-permute-start.10 = (f32[64,768]{1,0:T(8,128)S(1)}, f32[64,768]{1,0:T(8,128)S(1)}, u32[]{:S(2)}, u32[]{:S(2)}) collective-permute-start(f32[64,768]{1,0:T(8,128)S(1)} %bitcast_add_fusion.28), channel_id=1, source_target_pairs={{0,16},{1,17},{2,18},{3,19},{4,20},{5,21},{6,22},{7,23},{8,24},{9,... | collective-permute-start | bytes 589832 | tf_op jit(solution)/shard_map/ppermute | solution.py:54
  572.1 5.6 collective-permute-start.33
  573.7 5.7 collective-permute-start.14
  574.5 5.4 collective-permute-start.37
  577.7 5.6 collective-permute-start.34
  577.8 5.6 collective-permute-start.18
  579.4 6.8 %collective-permute-start.15 = (f32[16,768]{1,0:T(8,128)S(1)}, f32[16,768]{1,0:T(8,128)S(1)}, u32[]{:S(2)}, u32[]{:S(2)}) collective-permute-start(f32[16,768]{1,0:T(8,128)S(1)} %bitcast_add_fusion.47), channel_id=1, source_target_pairs={{0,1},{1,2},{2,3},{3,0},{4,5},{5,6},{6,7},{7,4},{8,9},{9,10},{10,1... | collective-permute-start | bytes 147464 | tf_op jit(solution)/shard_map/ppermute | solution.py:54
  580.0 6.3 %collective-permute-start.38 = (f32[16,768]{1,0:T(8,128)S(1)}, f32[16,768]{1,0:T(8,128)S(1)}, u32[]{:S(2)}, u32[]{:S(2)}) collective-permute-start(f32[16,768]{1,0:T(8,128)S(1)} %bitcast_add_fusion.37), channel_id=1, source_target_pairs={{0,96},{8,104},{16,112},{24,120},{32,0},{40,8},{48,16},{56,24},{64... | collective-permute-start | bytes 147464 | tf_op jit(solution)/shard_map/ppermute | solution.py:55
  583.3 5.4 collective-permute-start.35
  586.2 5.4 collective-permute-start.16
  (38 other events, 325.3 us)

commit v3 on v1

--- a/solution.py
+++ b/solution.py
@@ -33,6 +33,84 @@
 
 def apply_map(matrix, state):
     return jnp.einsum("thkr,trhd->tkhd", matrix, state, precision=lax.Precision.HIGHEST)
+
+
+def shifted(size, move):
+    return [(i, move(i)) for i in range(size)]
+
+
+def reduction_plan(seg_size, dp_size):
+    x_n, z_n = seg_size // 4, dp_size // 2
+
+    def y_move(sign):
+        def move(i):
+            s, d = divmod(i, dp_size)
+            y = (2 * (d // z_n) + (s // 2) % 2 + sign) % 4
+            return ((s // 4) * 4 + (y % 2) * 2 + s % 2) * dp_size + (y // 2) * z_n + d % z_n
+        return move
+
+    perms = {
+        "x": [shifted(seg_size, lambda i, g=g: ((i // 4 + g) % x_n) * 4 + i % 4) for g in (1, -1)],
+        "z": [shifted(dp_size, lambda i, g=g: (i // z_n) * z_n + (i % z_n + g) % z_n) for g in (1, -1)],
+        "y": [shifted(seg_size * dp_size, y_move(g)) for g in (1, -1)],
+        "core": shifted(seg_size, lambda i: i ^ 1),
+    }
+    axes = {"x": "seg", "z": "dp", "y": ("seg", "dp")}
+    return perms, axes
+
+
+ORDERS = (("x", "y", "z"), ("y", "z", "x"), ("z", "x", "y"))
+
+
+def feature_order(array, order, seg_size, dp_size):
+    lead = array.shape[:-1]
+    x_n, z_n = seg_size // 4, dp_size // 2
+    split = array.reshape(*lead, x_n, 2, 2, 2, z_n, -1)
+    n = len(lead)
+    place = {"x": [n], "y": [n + 3, n + 1], "z": [n + 4], "core": [n + 2]}
+    axes = list(range(n)) + place["core"] + [a for dim in order for a in place[dim]] + [n + 5]
+    return split.transpose(axes).reshape(array.shape)
+
+
+def reduce_colours(parts, where):
+    perms, axes = reduction_plan(lax.axis_size("seg"), lax.axis_size("dp"))
+    core = where["core"]
+    staged = []
+    for part in parts:
+        half = part.shape[0] // 2
+        send = lax.dynamic_slice_in_dim(part, (1 - core) * half, half, 0)
+        keep = lax.dynamic_slice_in_dim(part, core * half, half, 0)
+        staged.append((keep, lax.ppermute(send, "seg", perms["core"])))
+    parts = [keep + got for keep, got in staged]
+    for stage in range(3):
+        dims = [order[stage] for order in ORDERS]
+        split = []
+        for part in parts:
+            rows, cols = part.shape
+            quarter = part.reshape(4, 2, rows // 8, cols)
+            split.append((quarter[:, 0], quarter[:, 1]))
+
+        def own(block, index):
+            return lax.dynamic_index_in_dim(block, index % 4, 0, keepdims=False)
+
+        acc = [
+            [own(ahead, where[dim] - 1), own(behind, where[dim] + 1)]
+            for dim, (ahead, behind) in zip(dims, split)
+        ]
+        for step in (2, 3, 4):
+            moved = [
+                (
+                    lax.ppermute(a, axes[dim], perms[dim][0]),
+                    lax.ppermute(b, axes[dim], perms[dim][1]),
+                )
+                for dim, (a, b) in zip(dims, acc)
+            ]
+            acc = [
+                [a + own(ahead, where[dim] - step), b + own(behind, where[dim] + step)]
+                for dim, (a, b), (ahead, behind) in zip(dims, moved, split)
+            ]
+        parts = [jnp.concatenate(pair, axis=0) for pair in acc]
+    return parts
 
 
 def local(hidden, norm_gain, value_weight, queries, token_keys, summary_keys, output_grad):
@@ -67,9 +145,6 @@
     normed = hidden_f * inv_rms
     gain_f = norm_gain.astype(jnp.float32)
     scaled = (normed * gain_f).astype(jnp.bfloat16).reshape(trace_count * row_count, model_width)
-    weight_grad = lax.dot_general(
-        scaled, value_grad, (((0,), (0,)), ((), ())), preferred_element_type=jnp.float32
-    )
     normalized_gradient = lax.dot_general(
         value_grad, value_weight, (((1,), (1,)), ((), ())), preferred_element_type=jnp.float32
     )
@@ -81,10 +156,32 @@
     hidden_grad = inv_rms * (
         scaled_grad - normed * jnp.mean(scaled_grad * normed, axis=-1, keepdims=True)
     )
-    gain_block = jnp.zeros((model_width, 128), jnp.float32).at[:, 0].set(gain_grad)
-    both = jnp.concatenate([weight_grad, gain_block], axis=1)
-    both = lax.psum_scatter(both, "seg", scatter_dimension=0, tiled=True)
-    both = lax.psum_scatter(both, "dp", scatter_dimension=0, tiled=True)
+    seg_index, dp_index = lax.axis_index("seg"), lax.axis_index("dp")
+    z_n = lax.axis_size("dp") // 2
+    where = {
+        "x": seg_index // 4,
+        "y": 2 * (dp_index // z_n) + (seg_index // 2) % 2,
+        "z": dp_index % z_n,
+        "core": seg_index % 2,
+    }
+    seg_size, dp_size = lax.axis_size("seg"), lax.axis_size("dp")
+    bounds = (0, 768, 1536, value_width)
+    parts = []
+    for color, order in enumerate(ORDERS):
+        columns = value_grad[:, bounds[color] : bounds[color + 1]]
+        part = lax.dot_general(
+            feature_order(scaled, order, seg_size, dp_size),
+            columns,
+            (((0,), (0,)), ((), ())),
+            preferred_element_type=jnp.float32,
+        )
+        if color == len(ORDERS) - 1:
+            gain_col = feature_order(gain_grad, order, seg_size, dp_size)
+            gain_block = jnp.zeros((model_width, 128), jnp.float32).at[:, 0].set(gain_col)
+            part = jnp.concatenate([part, gain_block], axis=1)
+        parts.append(part)
+    pieces = reduce_colours(parts, where)
+    both = jnp.concatenate(pieces, axis=1)
     weight_part, gain_part = both[:, :value_width], both[:, value_width]
     return (hidden_grad.astype(jnp.bfloat16), summary_grad, weight_part, gain_part)
 

time: 719 us -> 518 us (0.72); the launches traced: 718 us -> 508 us
  waiting for transfers between devices: 574 us -> 220 us
  starting transfers between devices: 19.5 us -> 104 us
  local copies, waits for them, and re-layouts: 15.6 us -> 80.1 us
  other arithmetic: 39.3 us -> 51.6 us
  between operations: 14.2 us -> 2.06 us
    reduce_scatter x1 -> x0, waiting for transfers between devices: 382 us -> none  [local(): both = lax.psum_scatter(both, 'seg', scatter_dimension=0, tiled=True)]
    ppermute x0 -> x57, waiting for transfers between devices: none -> 102 us  [the longest x27 56.2 us: reduce_colours(): lax.ppermute(a, axes[dim], perms[dim][0])]
    ppermute x0 -> x57, starting transfers between devices: none -> 84.4 us  [the longest x27 62 us: reduce_colours(): lax.ppermute(b, axes[dim], perms[dim][1])]
    unnamed x3 -> x0, waiting for transfers between devices: 73.8 us -> none
    dynamic_slice x0 -> x13, local copies, waits for them, and re-layouts: none -> 33.4 us  [the longest x10 21.4 us: own(): return lax.dynamic_index_in_dim(block, index % 4, 0, keepdims=False)]
    add x0 -> x57, other arithmetic: none -> 28.1 us  [the longest x3 17.6 us: reduce_colours(): parts = [keep + got for keep, got in staged]]
    concatenate x1 -> x8, other arithmetic: 23.4 us -> 6.19 us  [the longest x1 5.1 us: local(): part = jnp.concatenate([part, gain_block], axis=1)]
    slice x2 -> x9, local copies, waits for them, and re-layouts: 2.39 us -> 11.8 us  [reduce_colours(): split.append((quarter[:, 0], quarter[:, 1]))]
  transfers between devices with their start and end apart: 17 -> 72, of which waited for: 17 -> 40; matrix products, arithmetic and copies ran while one was open for 1% -> 19% of each run, Pallas kernels for 0% -> 0%
where the time goes in v3:
time: 518 us; the launch traced here: 508 us
  waiting for transfers between devices  220 us (42%)
  starting transfers between devices  104 us (20%)
  local copies, waits for them, and re-layouts  80.1 us (15%)
  other arithmetic  51.6 us (10%)
  matrix products  50.8 us (10%)
    ppermute x15, waiting for transfers between devices, passed_along(): return lax.ppermute(block, axis, route)  118 us
    ppermute x27, starting transfers between devices, reduce_colours(): lax.ppermute(b, axes[dim], perms[dim][1])  62 us
    ppermute x27, waiting for transfers between devices, reduce_colours(): lax.ppermute(a, axes[dim], perms[dim][0])  56.2 us
    ppermute x27, waiting for transfers between devices, reduce_colours(): lax.ppermute(b, axes[dim], perms[dim][1])  45.5 us
    dynamic_slice x10, local copies, waits for them, and re-layouts, own(): return lax.dynamic_index_in_dim(block, index % 4, 0, keepdims=False)  21.4 us
    ppermute x15, starting transfers between devices, passed_along(): return lax.ppermute(block, axis, route)  19.4 us
    add x3, other arithmetic, reduce_colours(): parts = [keep + got for keep, got in staged]  17.6 us
    dot_general x16, matrix products, apply_map(): jnp.einsum('thkr,trhd->tkhd', matrix, state, precision=lax.Precision.HIGH...  17.1 us
  transfers between devices with their start and end apart: 72, of which 40 were waited for; matrix products, arithmetic and copies ran while one was open for 19% of the time, Pallas kernels for 0%

profile of v3, /device:TPU:0, one launch (start us, length us, event | category | flops | bytes accessed | tf_op | source)
XLA Modules:
  0.0 508.5 jit_solution(10593167471008348798)
XLA Ops:
  10.0 4.6 fusion.49
  15.9 4.5 convolution_bitcast_fusion.1
  21.7 154.3 %while.11 = (s32[]{:T(128)}, f32[1,50,16,128]{3,2,0,1:T(8,128)S(1)}, f32[1,16,50,50]{3,2,1,0:T(8,128)S(1)}, f32[1,50,16,128]{3,1,2,0:T(8,128)S(1)}, s32[]{:T(128)}) while((s32[]{:T(128)}, f32[1,50,16,128]{3,2,0,1:T(8,128)S(1)}, f32[1,16,50,50]{3,2,1,0:T(8,128)S(1)}, f32[1,50,16,128]{3,1,2,0:T(8,128)S(1)}, s32[]{:T(128)}) %tuple.47), condition=%wide.region_4.5_spmd, body=%wide.region_3.4_spmd.sunk | while | flops 61542400 | bytes 3846501 | solution.py:136
  28.9 7.5 %collective-permute-done = f32[1,50,2048]{2,0,1:T(1,128)S(1)} collective-permute-done((f32[1,50,2048]{2,0,1:T(1,128)S(1)}, f32[1,50,2048]{2,0,1:T(1,128)S(1)}, u32[]{:S(2)}, u32[]{:S(2)}) %collective-permute-start) | collective-permute-done | bytes 409632 | tf_op jit(solution)/shard_map/while/body/eval_jaxpr/ppermute | solution.py:13
  38.9 8.0 %collective-permute-done = f32[1,50,2048]{2,0,1:T(1,128)S(1)} collective-permute-done((f32[1,50,2048]{2,0,1:T(1,128)S(1)}, f32[1,50,2048]{2,0,1:T(1,128)S(1)}, u32[]{:S(2)}, u32[]{:S(2)}) %collective-permute-start) | collective-permute-done | bytes 409632 | tf_op jit(solution)/shard_map/while/body/eval_jaxpr/ppermute | solution.py:13
  49.2 8.0 %collective-permute-done = f32[1,50,2048]{2,0,1:T(1,128)S(1)} collective-permute-done((f32[1,50,2048]{2,0,1:T(1,128)S(1)}, f32[1,50,2048]{2,0,1:T(1,128)S(1)}, u32[]{:S(2)}, u32[]{:S(2)}) %collective-permute-start) | collective-permute-done | bytes 409632 | tf_op jit(solution)/shard_map/while/body/eval_jaxpr/ppermute | solution.py:13
  59.6 8.0 %collective-permute-done = f32[1,50,2048]{2,0,1:T(1,128)S(1)} collective-permute-done((f32[1,50,2048]{2,0,1:T(1,128)S(1)}, f32[1,50,2048]{2,0,1:T(1,128)S(1)}, u32[]{:S(2)}, u32[]{:S(2)}) %collective-permute-start) | collective-permute-done | bytes 409632 | tf_op jit(solution)/shard_map/while/body/eval_jaxpr/ppermute | solution.py:13
  70.0 8.0 %collective-permute-done = f32[1,50,2048]{2,0,1:T(1,128)S(1)} collective-permute-done((f32[1,50,2048]{2,0,1:T(1,128)S(1)}, f32[1,50,2048]{2,0,1:T(1,128)S(1)}, u32[]{:S(2)}, u32[]{:S(2)}) %collective-permute-start) | collective-permute-done | bytes 409632 | tf_op jit(solution)/shard_map/while/body/eval_jaxpr/ppermute | solution.py:13
  80.4 8.0 %collective-permute-done = f32[1,50,2048]{2,0,1:T(1,128)S(1)} collective-permute-done((f32[1,50,2048]{2,0,1:T(1,128)S(1)}, f32[1,50,2048]{2,0,1:T(1,128)S(1)}, u32[]{:S(2)}, u32[]{:S(2)}) %collective-permute-start) | collective-permute-done | bytes 409632 | tf_op jit(solution)/shard_map/while/body/eval_jaxpr/ppermute | solution.py:13
  90.8 8.0 %collective-permute-done = f32[1,50,2048]{2,0,1:T(1,128)S(1)} collective-permute-done((f32[1,50,2048]{2,0,1:T(1,128)S(1)}, f32[1,50,2048]{2,0,1:T(1,128)S(1)}, u32[]{:S(2)}, u32[]{:S(2)}) %collective-permute-start) | collective-permute-done | bytes 409632 | tf_op jit(solution)/shard_map/while/body/eval_jaxpr/ppermute | solution.py:13
  101.2 8.0 %collective-permute-done = f32[1,50,2048]{2,0,1:T(1,128)S(1)} collective-permute-done((f32[1,50,2048]{2,0,1:T(1,128)S(1)}, f32[1,50,2048]{2,0,1:T(1,128)S(1)}, u32[]{:S(2)}, u32[]{:S(2)}) %collective-permute-start) | collective-permute-done | bytes 409632 | tf_op jit(solution)/shard_map/while/body/eval_jaxpr/ppermute | solution.py:13
  111.5 8.0 %collective-permute-done = f32[1,50,2048]{2,0,1:T(1,128)S(1)} collective-permute-done((f32[1,50,2048]{2,0,1:T(1,128)S(1)}, f32[1,50,2048]{2,0,1:T(1,128)S(1)}, u32[]{:S(2)}, u32[]{:S(2)}) %collective-permute-start) | collective-permute-done | bytes 409632 | tf_op jit(solution)/shard_map/while/body/eval_jaxpr/ppermute | solution.py:13
  121.9 8.8 %collective-permute-done = f32[1,50,2048]{2,0,1:T(1,128)S(1)} collective-permute-done((f32[1,50,2048]{2,0,1:T(1,128)S(1)}, f32[1,50,2048]{2,0,1:T(1,128)S(1)}, u32[]{:S(2)}, u32[]{:S(2)}) %collective-permute-start) | collective-permute-done | bytes 409632 | tf_op jit(solution)/shard_map/while/body/eval_jaxpr/ppermute | solution.py:13
  133.2 8.9 %collective-permute-done = f32[1,50,2048]{2,0,1:T(1,128)S(1)} collective-permute-done((f32[1,50,2048]{2,0,1:T(1,128)S(1)}, f32[1,50,2048]{2,0,1:T(1,128)S(1)}, u32[]{:S(2)}, u32[]{:S(2)}) %collective-permute-start) | collective-permute-done | bytes 409632 | tf_op jit(solution)/shard_map/while/body/eval_jaxpr/ppermute | solution.py:13
  144.5 8.9 %collective-permute-done = f32[1,50,2048]{2,0,1:T(1,128)S(1)} collective-permute-done((f32[1,50,2048]{2,0,1:T(1,128)S(1)}, f32[1,50,2048]{2,0,1:T(1,128)S(1)}, u32[]{:S(2)}, u32[]{:S(2)}) %collective-permute-start) | collective-permute-done | bytes 409632 | tf_op jit(solution)/shard_map/while/body/eval_jaxpr/ppermute | solution.py:13
  155.7 8.9 %collective-permute-done = f32[1,50,2048]{2,0,1:T(1,128)S(1)} collective-permute-done((f32[1,50,2048]{2,0,1:T(1,128)S(1)}, f32[1,50,2048]{2,0,1:T(1,128)S(1)}, u32[]{:S(2)}, u32[]{:S(2)}) %collective-permute-start) | collective-permute-done | bytes 409632 | tf_op jit(solution)/shard_map/while/body/eval_jaxpr/ppermute | solution.py:13
  167.0 8.9 %collective-permute-done = f32[1,50,2048]{2,0,1:T(1,128)S(1)} collective-permute-done((f32[1,50,2048]{2,0,1:T(1,128)S(1)}, f32[1,50,2048]{2,0,1:T(1,128)S(1)}, u32[]{:S(2)}, u32[]{:S(2)}) %collective-permute-start) | collective-permute-done | bytes 409632 | tf_op jit(solution)/shard_map/while/body/eval_jaxpr/ppermute | solution.py:13
  176.0 4.2 fusion.19
  182.5 12.6 %fusion.14 = (f32[4096]{0:T(1024)S(1)}, f32[320]{0:T(512)}, bf16[1,320,4096]{2,1,0:T(8,128)(2,1)}, f32[320,4096]{1,0:T(8,128)}) fusion(bf16[1,320,4096]{2,1,0:T(8,128)(2,1)S(1)} %copy-done.6, f32[320]{0:T(512)S(1)} %add_rsqrt_fusion, f32[4096]{0:T(1024)S(1)} %convert_element_type.26, bf16[4096,2048]{1,0:T(8,128)(2,1)} %param.13, ...), kind=kOutput, calls=%fused_computation.24 | convolution fusion | flops 5380500992 | bytes 28609024 | tf_op jit(solution)/shard_map/dot_general | solution.py:148
  196.6 3.3 copy.38
  202.3 4.3 fusion.30
  206.6 5.1 %select_maximum_fusion = f32[4096,640]{0,1:T(8,128)} fusion(f32[4096,1]{0,1:T(1,128)S(1)} %copy-done.24, f32[4096,512]{0,1:T(8,128)S(1)} %fusion.30), kind=kLoop, calls=%fused_computation.5 | loop fusion | flops 7864320 | bytes 18890752 | tf_op jit(solution)/shard_map/concatenate | solution.py:181
  211.7 5.4 %constant_dynamic-slice_fusion.8 = f32[2048,640]{0,1:T(8,128)} fusion(f32[4096,640]{0,1:T(8,128)} %select_maximum_fusion, s32[]{:T(128)S(6)} %select_n.361), kind=kLoop, calls=%fused_computation.142 | loop fusion | bytes 10485764 | tf_op jit(solution)/shard_map/dynamic_slice | solution.py:81
  217.2 7.2 %collective-permute-start.39 = (f32[2048,640]{0,1:T(8,128)}, f32[2048,640]{0,1:T(8,128)}, u32[]{:S(2)}, u32[]{:S(2)}) collective-permute-start(f32[2048,640]{0,1:T(8,128)} %constant_dynamic-slice_fusion.8), channel_id=1, source_target_pairs={{0,8},{8,0},{16,24},{24,16},{32,40},{40,32},{48,56},{56,48},{64,72... | collective-permute-start | bytes 15728648 | tf_op jit(solution)/shard_map/ppermute | solution.py:83
  225.7 3.5 fusion.24
  229.2 3.3 constant_dynamic-slice_fusion.9
  232.5 3.2 copy-done.1
  236.1 3.5 fusion.26
  239.6 3.3 constant_dynamic-slice_fusion.10
  242.9 3.2 copy-done
  246.9 7.9 %dynamic-slice_add_fusion.2 = f32[2048,640]{0,1:T(8,128)} fusion(f32[2048,640]{0,1:T(8,128)} %collective-permute-done.39, f32[4096,640]{0,1:T(8,128)} %select_maximum_fusion, s32[]{:T(128)S(6)} %select_n.360), kind=kLoop, calls=%fused_computation.26 | loop fusion | flops 1310720 | bytes 15728644 | tf_op jit(solution)/shard_map/add | solution.py:84
  254.8 8.1 %reshape.353 = f32[4,2,256,640]{2,1,0,3:T(2,128)} reshape(f32[2048,640]{0,1:T(8,128)} %dynamic-slice_add_fusion.2) | data formatting | bytes 10485760 | tf_op jit(solution)/shard_map/reshape | solution.py:90
  262.9 10.0 %fusion.42 = (f32[4,1,256,640]{2,1,0,3:T(1,128)S(1)}, f32[4,1,256,640]{2,1,0,3:T(1,128)}) fusion(f32[4,2,256,640]{2,1,0,3:T(2,128)} %reshape.353), kind=kLoop, calls=%fused_computation.157 | loop fusion | bytes 10485760 | tf_op jit(solution)/shard_map/slice | solution.py:91
  273.0 4.7 constant_dynamic-slice_fusion
  279.8 4.0 collective-permute-start.43
  283.8 3.1 constant_dynamic-slice_fusion.4
  289.1 6.3 %fusion.12 = bf16[1,320,4096]{2,1,0:T(8,128)(2,1)} fusion(bf16[1,320,4096]{2,1,0:T(8,128)(2,1)} %param.11, f32[320,4096]{1,0:T(8,128)} %get-tuple-element.86, f32[320]{0:T(512)S(1)} %broadcast_multiply_fusion, f32[4096]{0:T(1024)S(1)} %copy-done.23, f32[320]{0:T(512)S(1)} %copy-done.26), kind=kLoop, calls=%fused_computation.22 | loop fusion | flops 9175040 | bytes 10504704 | tf_op jit(solution)/shard_map/convert_element_type | solution.py:186
  309.7 3.2 collective-permute-start.44
  314.9 5.6 %dynamic-slice_add_fusion = f32[2048,768]{1,0:T(8,128)S(1)} fusion(f32[2048,768]{1,0:T(8,128)} %collective-permute-done.20, f32[4096,768]{1,0:T(8,128)} %copy-done.1, s32[]{:T(128)S(6)} %select_n.360), kind=kLoop, calls=%fused_computation.16 | loop fusion | flops 1572864 | bytes 18874372 | tf_op jit(solution)/shard_map/add | solution.py:84
  322.2 11.0 %collective-permute-start.24 = (f32[256,768]{1,0:T(8,128)}, f32[256,768]{1,0:T(8,128)}, u32[]{:S(2)}, u32[]{:S(2)}) collective-permute-start(f32[256,768]{1,0:T(8,128)} %dynamic-slice_bitcast_fusion), channel_id=1, source_target_pairs={{0,20},{1,21},{2,22},{3,23},{4,16},{5,17},{6,18},{7,19},{8,28},{9,... | collective-permute-start | bytes 2359304 | tf_op jit(solution)/shard_map/ppermute | solution.py:104
  334.1 4.1 dynamic-slice_add_fusion.1
  342.4 3.3 collective-permute-start.45
  346.9 2.9 collective-permute-done.24
  351.0 3.1 collective-permute-done.21
  361.1 5.0 collective-permute-done.42
  368.7 11.8 %collective-permute-done.49 = f32[64,640]{1,0:T(8,128)S(1)} collective-permute-done((f32[64,640]{1,0:T(8,128)S(1)}, f32[64,640]{1,0:T(8,128)S(1)}, u32[]{:S(2)}, u32[]{:S(2)}) %collective-permute-start.49) | collective-permute-done | bytes 163872 | tf_op jit(solution)/shard_map/ppermute | solution.py:104
  381.9 7.5 %collective-permute-done.46 = f32[64,640]{1,0:T(8,128)S(1)} collective-permute-done((f32[64,640]{1,0:T(8,128)S(1)}, f32[64,640]{1,0:T(8,128)S(1)}, u32[]{:S(2)}, u32[]{:S(2)}) %collective-permute-start.46) | collective-permute-done | bytes 163872 | tf_op jit(solution)/shard_map/ppermute | solution.py:103
  390.4 4.3 collective-permute-done.50
  394.8 6.5 %collective-permute-done.47 = f32[64,640]{1,0:T(8,128)S(1)} collective-permute-done((f32[64,640]{1,0:T(8,128)S(1)}, f32[64,640]{1,0:T(8,128)S(1)}, u32[]{:S(2)}, u32[]{:S(2)}) %collective-permute-start.47) | collective-permute-done | bytes 163872 | tf_op jit(solution)/shard_map/ppermute | solution.py:103
  402.3 4.3 collective-permute-done.51
  406.6 6.5 %collective-permute-done.48 = f32[64,640]{1,0:T(8,128)S(1)} collective-permute-done((f32[64,640]{1,0:T(8,128)S(1)}, f32[64,640]{1,0:T(8,128)S(1)}, u32[]{:S(2)}, u32[]{:S(2)}) %collective-permute-start.48) | collective-permute-done | bytes 163872 | tf_op jit(solution)/shard_map/ppermute | solution.py:103
  413.2 3.0 collective-permute-start.55
  419.0 4.4 collective-permute-done.52
  427.4 5.2 %collective-permute-done.53 = f32[16,640]{1,0:T(8,128)S(1)} collective-permute-done((f32[16,640]{1,0:T(8,128)S(1)}, f32[16,640]{1,0:T(8,128)S(1)}, u32[]{:S(2)}, u32[]{:S(2)}) %collective-permute-start.53) | collective-permute-done | bytes 40992 | tf_op jit(solution)/shard_map/ppermute | solution.py:103
  437.1 5.8 %collective-permute-done.54 = f32[16,640]{1,0:T(8,128)S(1)} collective-permute-done((f32[16,640]{1,0:T(8,128)S(1)}, f32[16,640]{1,0:T(8,128)S(1)}, u32[]{:S(2)}, u32[]{:S(2)}) %collective-permute-start.54) | collective-permute-done | bytes 40992 | tf_op jit(solution)/shard_map/ppermute | solution.py:103
  448.3 11.6 %collective-permute-done.26 = f32[256,768]{1,0:T(8,128)S(1)} collective-permute-done((f32[256,768]{1,0:T(8,128)S(1)}, f32[256,768]{1,0:T(8,128)S(1)}, u32[]{:S(2)}, u32[]{:S(2)}) %collective-permute-start.26) | collective-permute-done | bytes 786464 | tf_op jit(solution)/shard_map/ppermute | solution.py:104
  460.0 3.0 collective-permute-done.23
  474.9 3.2 collective-permute-start.32
  481.6 4.0 collective-permute-done.29
  490.3 3.3 collective-permute-start.37
  495.9 3.3 collective-permute-start.38
  499.3 2.6 collective-permute-start.19
  502.0 2.5 collective-permute-done.35
  504.6 2.7 collective-permute-done.16
  (316 shorter events, 141.4 us)
Async XLA Ops:
  27.6 8.8 %collective-permute-start = (f32[1,50,2048]{2,0,1:T(1,128)S(1)}, f32[1,50,2048]{2,0,1:T(1,128)S(1)}, u32[]{:S(2)}, u32[]{:S(2)}) collective-permute-start(f32[1,50,2048]{2,0,1:T(1,128)S(1)} %bitcast.264), channel_id=1, source_target_pairs={{8,0},{16,8},{24,16},{32,24},{40,32},{48,40},{56,48},{64,56},{72,6... | collective-permute-start | bytes 1228808 | tf_op jit(solution)/shard_map/while/body/eval_jaxpr/ppermute | solution.py:13
  37.6 9.3 %collective-permute-start = (f32[1,50,2048]{2,0,1:T(1,128)S(1)}, f32[1,50,2048]{2,0,1:T(1,128)S(1)}, u32[]{:S(2)}, u32[]{:S(2)}) collective-permute-start(f32[1,50,2048]{2,0,1:T(1,128)S(1)} %bitcast.264), channel_id=1, source_target_pairs={{8,0},{16,8},{24,16},{32,24},{40,32},{48,40},{56,48},{64,56},{72,6... | collective-permute-start | bytes 1228808 | tf_op jit(solution)/shard_map/while/body/eval_jaxpr/ppermute | solution.py:13
  47.9 9.3 %collective-permute-start = (f32[1,50,2048]{2,0,1:T(1,128)S(1)}, f32[1,50,2048]{2,0,1:T(1,128)S(1)}, u32[]{:S(2)}, u32[]{:S(2)}) collective-permute-start(f32[1,50,2048]{2,0,1:T(1,128)S(1)} %bitcast.264), channel_id=1, source_target_pairs={{8,0},{16,8},{24,16},{32,24},{40,32},{48,40},{56,48},{64,56},{72,6... | collective-permute-start | bytes 1228808 | tf_op jit(solution)/shard_map/while/body/eval_jaxpr/ppermute | solution.py:13
  58.3 9.3 %collective-permute-start = (f32[1,50,2048]{2,0,1:T(1,128)S(1)}, f32[1,50,2048]{2,0,1:T(1,128)S(1)}, u32[]{:S(2)}, u32[]{:S(2)}) collective-permute-start(f32[1,50,2048]{2,0,1:T(1,128)S(1)} %bitcast.264), channel_id=1, source_target_pairs={{8,0},{16,8},{24,16},{32,24},{40,32},{48,40},{56,48},{64,56},{72,6... | collective-permute-start | bytes 1228808 | tf_op jit(solution)/shard_map/while/body/eval_jaxpr/ppermute | solution.py:13
  68.7 9.3 %collective-permute-start = (f32[1,50,2048]{2,0,1:T(1,128)S(1)}, f32[1,50,2048]{2,0,1:T(1,128)S(1)}, u32[]{:S(2)}, u32[]{:S(2)}) collective-permute-start(f32[1,50,2048]{2,0,1:T(1,128)S(1)} %bitcast.264), channel_id=1, source_target_pairs={{8,0},{16,8},{24,16},{32,24},{40,32},{48,40},{56,48},{64,56},{72,6... | collective-permute-start | bytes 1228808 | tf_op jit(solution)/shard_map/while/body/eval_jaxpr/ppermute | solution.py:13
  79.1 9.3 %collective-permute-start = (f32[1,50,2048]{2,0,1:T(1,128)S(1)}, f32[1,50,2048]{2,0,1:T(1,128)S(1)}, u32[]{:S(2)}, u32[]{:S(2)}) collective-permute-start(f32[1,50,2048]{2,0,1:T(1,128)S(1)} %bitcast.264), channel_id=1, source_target_pairs={{8,0},{16,8},{24,16},{32,24},{40,32},{48,40},{56,48},{64,56},{72,6... | collective-permute-start | bytes 1228808 | tf_op jit(solution)/shard_map/while/body/eval_jaxpr/ppermute | solution.py:13
  89.5 9.3 %collective-permute-start = (f32[1,50,2048]{2,0,1:T(1,128)S(1)}, f32[1,50,2048]{2,0,1:T(1,128)S(1)}, u32[]{:S(2)}, u32[]{:S(2)}) collective-permute-start(f32[1,50,2048]{2,0,1:T(1,128)S(1)} %bitcast.264), channel_id=1, source_target_pairs={{8,0},{16,8},{24,16},{32,24},{40,32},{48,40},{56,48},{64,56},{72,6... | collective-permute-start | bytes 1228808 | tf_op jit(solution)/shard_map/while/body/eval_jaxpr/ppermute | solution.py:13
  99.8 9.3 %collective-permute-start = (f32[1,50,2048]{2,0,1:T(1,128)S(1)}, f32[1,50,2048]{2,0,1:T(1,128)S(1)}, u32[]{:S(2)}, u32[]{:S(2)}) collective-permute-start(f32[1,50,2048]{2,0,1:T(1,128)S(1)} %bitcast.264), channel_id=1, source_target_pairs={{8,0},{16,8},{24,16},{32,24},{40,32},{48,40},{56,48},{64,56},{72,6... | collective-permute-start | bytes 1228808 | tf_op jit(solution)/shard_map/while/body/eval_jaxpr/ppermute | solution.py:13
  110.2 9.3 %collective-permute-start = (f32[1,50,2048]{2,0,1:T(1,128)S(1)}, f32[1,50,2048]{2,0,1:T(1,128)S(1)}, u32[]{:S(2)}, u32[]{:S(2)}) collective-permute-start(f32[1,50,2048]{2,0,1:T(1,128)S(1)} %bitcast.264), channel_id=1, source_target_pairs={{8,0},{16,8},{24,16},{32,24},{40,32},{48,40},{56,48},{64,56},{72,6... | collective-permute-start | bytes 1228808 | tf_op jit(solution)/shard_map/while/body/eval_jaxpr/ppermute | solution.py:13
  120.6 10.1 %collective-permute-start = (f32[1,50,2048]{2,0,1:T(1,128)S(1)}, f32[1,50,2048]{2,0,1:T(1,128)S(1)}, u32[]{:S(2)}, u32[]{:S(2)}) collective-permute-start(f32[1,50,2048]{2,0,1:T(1,128)S(1)} %bitcast.264), channel_id=1, source_target_pairs={{8,0},{16,8},{24,16},{32,24},{40,32},{48,40},{56,48},{64,56},{72,6... | collective-permute-start | bytes 1228808 | tf_op jit(solution)/shard_map/while/body/eval_jaxpr/ppermute | solution.py:13
  131.9 10.2 %collective-permute-start = (f32[1,50,2048]{2,0,1:T(1,128)S(1)}, f32[1,50,2048]{2,0,1:T(1,128)S(1)}, u32[]{:S(2)}, u32[]{:S(2)}) collective-permute-start(f32[1,50,2048]{2,0,1:T(1,128)S(1)} %bitcast.264), channel_id=1, source_target_pairs={{8,0},{16,8},{24,16},{32,24},{40,32},{48,40},{56,48},{64,56},{72,6... | collective-permute-start | bytes 1228808 | tf_op jit(solution)/shard_map/while/body/eval_jaxpr/ppermute | solution.py:13
  143.2 10.2 %collective-permute-start = (f32[1,50,2048]{2,0,1:T(1,128)S(1)}, f32[1,50,2048]{2,0,1:T(1,128)S(1)}, u32[]{:S(2)}, u32[]{:S(2)}) collective-permute-start(f32[1,50,2048]{2,0,1:T(1,128)S(1)} %bitcast.264), channel_id=1, source_target_pairs={{8,0},{16,8},{24,16},{32,24},{40,32},{48,40},{56,48},{64,56},{72,6... | collective-permute-start | bytes 1228808 | tf_op jit(solution)/shard_map/while/body/eval_jaxpr/ppermute | solution.py:13
  154.4 10.2 %collective-permute-start = (f32[1,50,2048]{2,0,1:T(1,128)S(1)}, f32[1,50,2048]{2,0,1:T(1,128)S(1)}, u32[]{:S(2)}, u32[]{:S(2)}) collective-permute-start(f32[1,50,2048]{2,0,1:T(1,128)S(1)} %bitcast.264), channel_id=1, source_target_pairs={{8,0},{16,8},{24,16},{32,24},{40,32},{48,40},{56,48},{64,56},{72,6... | collective-permute-start | bytes 1228808 | tf_op jit(solution)/shard_map/while/body/eval_jaxpr/ppermute | solution.py:13
  165.7 10.2 %collective-permute-start = (f32[1,50,2048]{2,0,1:T(1,128)S(1)}, f32[1,50,2048]{2,0,1:T(1,128)S(1)}, u32[]{:S(2)}, u32[]{:S(2)}) collective-permute-start(f32[1,50,2048]{2,0,1:T(1,128)S(1)} %bitcast.264), channel_id=1, source_target_pairs={{8,0},{16,8},{24,16},{32,24},{40,32},{48,40},{56,48},{64,56},{72,6... | collective-permute-start | bytes 1228808 | tf_op jit(solution)/shard_map/while/body/eval_jaxpr/ppermute | solution.py:13
  217.2 29.8 %collective-permute-start.39 = (f32[2048,640]{0,1:T(8,128)}, f32[2048,640]{0,1:T(8,128)}, u32[]{:S(2)}, u32[]{:S(2)}) collective-permute-start(f32[2048,640]{0,1:T(8,128)} %constant_dynamic-slice_fusion.8), channel_id=1, source_target_pairs={{0,8},{8,0},{16,24},{24,16},{32,40},{40,32},{48,56},{56,48},{64,72... | collective-permute-start | bytes 15728648 | tf_op jit(solution)/shard_map/ppermute | solution.py:83
  235.7 79.2 %collective-permute-start.20 = (f32[2048,768]{1,0:T(8,128)}, f32[2048,768]{1,0:T(8,128)}, u32[]{:S(2)}, u32[]{:S(2)}) collective-permute-start(f32[2048,768]{1,0:T(8,128)} %constant_dynamic-slice_fusion.9), channel_id=1, source_target_pairs={{0,8},{8,0},{16,24},{24,16},{32,40},{40,32},{48,56},{56,48},{64,72... | collective-permute-start | bytes 18874376 | tf_op jit(solution)/shard_map/ppermute | solution.py:83
  246.1 88.0 %collective-permute-start.1 = (f32[2048,768]{1,0:T(8,128)}, f32[2048,768]{1,0:T(8,128)}, u32[]{:S(2)}, u32[]{:S(2)}) collective-permute-start(f32[2048,768]{1,0:T(8,128)} %constant_dynamic-slice_fusion.10), channel_id=1, source_target_pairs={{0,8},{8,0},{16,24},{24,16},{32,40},{40,32},{48,56},{56,48},{64,72... | collective-permute-start | bytes 18874376 | tf_op jit(solution)/shard_map/ppermute | solution.py:83
  279.8 27.8 %collective-permute-start.43 = (f32[256,640]{1,0:T(8,128)}, f32[256,640]{1,0:T(8,128)}, u32[]{:S(2)}, u32[]{:S(2)}) collective-permute-start(f32[256,640]{1,0:T(8,128)} %bitcast.281), channel_id=1, source_target_pairs={{0,3},{1,0},{2,1},{3,2},{4,7},{5,4},{6,5},{7,6},{8,11},{9,8},{10,9... | collective-permute-start | bytes 1966088 | tf_op jit(solution)/shard_map/ppermute | solution.py:104
  288.9 23.9 %collective-permute-start.40 = (f32[256,640]{1,0:T(8,128)}, f32[256,640]{1,0:T(8,128)}, u32[]{:S(2)}, u32[]{:S(2)}) collective-permute-start(f32[256,640]{1,0:T(8,128)} %bitcast.87), channel_id=1, source_target_pairs={{0,1},{1,2},{2,3},{3,0},{4,5},{5,6},{6,7},{7,4},{8,9},{9,10},{10,1... | collective-permute-start | bytes 1966088 | tf_op jit(solution)/shard_map/ppermute | solution.py:103
  309.7 30.5 %collective-permute-start.44 = (f32[256,640]{1,0:T(8,128)}, f32[256,640]{1,0:T(8,128)}, u32[]{:S(2)}, u32[]{:S(2)}) collective-permute-start(f32[256,640]{1,0:T(8,128)} %bitcast_add_fusion.14), channel_id=1, source_target_pairs={{0,3},{1,0},{2,1},{3,2},{4,7},{5,4},{6,5},{7,6},{8,11},{9,8},{10,9... | collective-permute-start | bytes 1966088 | tf_op jit(solution)/shard_map/ppermute | solution.py:104
  314.9 27.6 %collective-permute-start.41 = (f32[256,640]{1,0:T(8,128)}, f32[256,640]{1,0:T(8,128)}, u32[]{:S(2)}, u32[]{:S(2)}) collective-permute-start(f32[256,640]{1,0:T(8,128)} %bitcast_add_fusion.17), channel_id=1, source_target_pairs={{0,1},{1,2},{2,3},{3,0},{4,5},{5,6},{6,7},{7,4},{8,9},{9,10},{10,1... | collective-permute-start | bytes 1966088 | tf_op jit(solution)/shard_map/ppermute | solution.py:103
  322.2 27.6 %collective-permute-start.24 = (f32[256,768]{1,0:T(8,128)}, f32[256,768]{1,0:T(8,128)}, u32[]{:S(2)}, u32[]{:S(2)}) collective-permute-start(f32[256,768]{1,0:T(8,128)} %dynamic-slice_bitcast_fusion), channel_id=1, source_target_pairs={{0,20},{1,21},{2,22},{3,23},{4,16},{5,17},{6,18},{7,19},{8,28},{9,... | collective-permute-start | bytes 2359304 | tf_op jit(solution)/shard_map/ppermute | solution.py:104
  334.1 20.1 %collective-permute-start.21 = (f32[256,768]{1,0:T(8,128)}, f32[256,768]{1,0:T(8,128)}, u32[]{:S(2)}, u32[]{:S(2)}) collective-permute-start(f32[256,768]{1,0:T(8,128)} %dynamic-slice_bitcast_fusion.1), channel_id=1, source_target_pairs={{0,16},{1,17},{2,18},{3,19},{4,20},{5,21},{6,22},{7,23},{8,24},{9,... | collective-permute-start | bytes 2359304 | tf_op jit(solution)/shard_map/ppermute | solution.py:103
  339.0 18.6 %collective-permute-start.5 = (f32[256,768]{1,0:T(8,128)S(1)}, f32[256,768]{1,0:T(8,128)S(1)}, u32[]{:S(2)}, u32[]{:S(2)}) collective-permute-start(f32[256,768]{1,0:T(8,128)S(1)} %dynamic-slice_bitcast_fusion.2), channel_id=1, source_target_pairs={{0,96},{8,104},{16,112},{24,120},{32,0},{40,8},{48,16},{56,24},{64... | collective-permute-start | bytes 2359304 | tf_op jit(solution)/shard_map/ppermute | solution.py:104
  340.2 27.5 %collective-permute-start.2 = (f32[256,768]{1,0:T(8,128)S(1)}, f32[256,768]{1,0:T(8,128)S(1)}, u32[]{:S(2)}, u32[]{:S(2)}) collective-permute-start(f32[256,768]{1,0:T(8,128)S(1)} %dynamic-slice_bitcast_fusion.3), channel_id=1, source_target_pairs={{0,32},{8,40},{16,48},{24,56},{32,64},{40,72},{48,80},{56,88},{64,... | collective-permute-start | bytes 2359304 | tf_op jit(solution)/shard_map/ppermute | solution.py:103
  342.4 16.6 %collective-permute-start.45 = (f32[256,640]{1,0:T(8,128)S(1)}, f32[256,640]{1,0:T(8,128)S(1)}, u32[]{:S(2)}, u32[]{:S(2)}) collective-permute-start(f32[256,640]{1,0:T(8,128)S(1)} %bitcast_add_fusion.13), channel_id=1, source_target_pairs={{0,3},{1,0},{2,1},{3,2},{4,7},{5,4},{6,5},{7,6},{8,11},{9,8},{10,9... | collective-permute-start | bytes 1966088 | tf_op jit(solution)/shard_map/ppermute | solution.py:104
  349.8 16.3 %collective-permute-start.42 = (f32[256,640]{1,0:T(8,128)S(1)}, f32[256,640]{1,0:T(8,128)S(1)}, u32[]{:S(2)}, u32[]{:S(2)}) collective-permute-start(f32[256,640]{1,0:T(8,128)S(1)} %bitcast_add_fusion.16), channel_id=1, source_target_pairs={{0,1},{1,2},{2,3},{3,0},{4,5},{5,6},{6,7},{7,4},{8,9},{9,10},{10,1... | collective-permute-start | bytes 1966088 | tf_op jit(solution)/shard_map/ppermute | solution.py:103
  354.1 89.4 %collective-permute-start.25 = (f32[256,768]{1,0:T(8,128)S(1)}, f32[256,768]{1,0:T(8,128)S(1)}, u32[]{:S(2)}, u32[]{:S(2)}) collective-permute-start(f32[256,768]{1,0:T(8,128)S(1)} %bitcast_add_fusion.2), channel_id=1, source_target_pairs={{0,20},{1,21},{2,22},{3,23},{4,16},{5,17},{6,18},{7,19},{8,28},{9,... | collective-permute-start | bytes 2359304 | tf_op jit(solution)/shard_map/ppermute | solution.py:104
  357.6 88.0 %collective-permute-start.22 = (f32[256,768]{1,0:T(8,128)S(1)}, f32[256,768]{1,0:T(8,128)S(1)}, u32[]{:S(2)}, u32[]{:S(2)}) collective-permute-start(f32[256,768]{1,0:T(8,128)S(1)} %bitcast_add_fusion.5), channel_id=1, source_target_pairs={{0,16},{1,17},{2,18},{3,19},{4,20},{5,21},{6,22},{7,23},{8,24},{9,... | collective-permute-start | bytes 2359304 | tf_op jit(solution)/shard_map/ppermute | solution.py:103
  359.0 86.9 %collective-permute-start.6 = (f32[256,768]{1,0:T(8,128)S(1)}, f32[256,768]{1,0:T(8,128)S(1)}, u32[]{:S(2)}, u32[]{:S(2)}) collective-permute-start(f32[256,768]{1,0:T(8,128)S(1)} %bitcast_add_fusion.8), channel_id=1, source_target_pairs={{0,96},{8,104},{16,112},{24,120},{32,0},{40,8},{48,16},{56,24},{64... | collective-permute-start | bytes 2359304 | tf_op jit(solution)/shard_map/ppermute | solution.py:104
  366.4 14.0 %collective-permute-start.49 = (f32[64,640]{1,0:T(8,128)S(1)}, f32[64,640]{1,0:T(8,128)S(1)}, u32[]{:S(2)}, u32[]{:S(2)}) collective-permute-start(f32[64,640]{1,0:T(8,128)S(1)} %dynamic-slice_bitcast_fusion.8), channel_id=1, source_target_pairs={{0,96},{8,104},{16,112},{24,120},{32,0},{40,8},{48,16},{56,24},{64... | collective-permute-start | bytes 491528 | tf_op jit(solution)/shard_map/ppermute | solution.py:104
  367.8 79.9 %collective-permute-start.3 = (f32[256,768]{1,0:T(8,128)S(1)}, f32[256,768]{1,0:T(8,128)S(1)}, u32[]{:S(2)}, u32[]{:S(2)}) collective-permute-start(f32[256,768]{1,0:T(8,128)S(1)} %bitcast_add_fusion.11), channel_id=1, source_target_pairs={{0,32},{8,40},{16,48},{24,56},{32,64},{40,72},{48,80},{56,88},{64,... | collective-permute-start | bytes 2359304 | tf_op jit(solution)/shard_map/ppermute | solution.py:103
  380.4 9.0 %collective-permute-start.46 = (f32[64,640]{1,0:T(8,128)S(1)}, f32[64,640]{1,0:T(8,128)S(1)}, u32[]{:S(2)}, u32[]{:S(2)}) collective-permute-start(f32[64,640]{1,0:T(8,128)S(1)} %dynamic-slice_bitcast_fusion.9), channel_id=1, source_target_pairs={{0,32},{8,40},{16,48},{24,56},{32,64},{40,72},{48,80},{56,88},{64,... | collective-permute-start | bytes 491528 | tf_op jit(solution)/shard_map/ppermute | solution.py:103
  394.7 6.5 %collective-permute-start.47 = (f32[64,640]{1,0:T(8,128)S(1)}, f32[64,640]{1,0:T(8,128)S(1)}, u32[]{:S(2)}, u32[]{:S(2)}) collective-permute-start(f32[64,640]{1,0:T(8,128)S(1)} %bitcast_add_fusion.35), channel_id=1, source_target_pairs={{0,32},{8,40},{16,48},{24,56},{32,64},{40,72},{48,80},{56,88},{64,... | collective-permute-start | bytes 491528 | tf_op jit(solution)/shard_map/ppermute | solution.py:103
  401.3 5.3 %collective-permute-start.51 = (f32[64,640]{1,0:T(8,128)S(1)}, f32[64,640]{1,0:T(8,128)S(1)}, u32[]{:S(2)}, u32[]{:S(2)}) collective-permute-start(f32[64,640]{1,0:T(8,128)S(1)} %bitcast_add_fusion.31), channel_id=1, source_target_pairs={{0,96},{8,104},{16,112},{24,120},{32,0},{40,8},{48,16},{56,24},{64... | collective-permute-start | bytes 491528 | tf_op jit(solution)/shard_map/ppermute | solution.py:104
  406.6 6.5 %collective-permute-start.48 = (f32[64,640]{1,0:T(8,128)S(1)}, f32[64,640]{1,0:T(8,128)S(1)}, u32[]{:S(2)}, u32[]{:S(2)}) collective-permute-start(f32[64,640]{1,0:T(8,128)S(1)} %bitcast_add_fusion.34), channel_id=1, source_target_pairs={{0,32},{8,40},{16,48},{24,56},{32,64},{40,72},{48,80},{56,88},{64,... | collective-permute-start | bytes 491528 | tf_op jit(solution)/shard_map/ppermute | solution.py:103
  417.9 5.5 %collective-permute-start.52 = (f32[16,640]{1,0:T(8,128)S(1)}, f32[16,640]{1,0:T(8,128)S(1)}, u32[]{:S(2)}, u32[]{:S(2)}) collective-permute-start(f32[16,640]{1,0:T(8,128)S(1)} %dynamic-slice_bitcast_fusion.15), channel_id=1, source_target_pairs={{0,16},{1,17},{2,18},{3,19},{4,20},{5,21},{6,22},{7,23},{8,24},{9,... | collective-permute-start | bytes 122888 | tf_op jit(solution)/shard_map/ppermute | solution.py:103
  437.1 5.8 %collective-permute-start.54 = (f32[16,640]{1,0:T(8,128)S(1)}, f32[16,640]{1,0:T(8,128)S(1)}, u32[]{:S(2)}, u32[]{:S(2)}) collective-permute-start(f32[16,640]{1,0:T(8,128)S(1)} %bitcast_add_fusion.52), channel_id=1, source_target_pairs={{0,16},{1,17},{2,18},{3,19},{4,20},{5,21},{6,22},{7,23},{8,24},{9,... | collective-permute-start | bytes 122888 | tf_op jit(solution)/shard_map/ppermute | solution.py:103
  443.6 16.3 %collective-permute-start.26 = (f32[256,768]{1,0:T(8,128)S(1)}, f32[256,768]{1,0:T(8,128)S(1)}, u32[]{:S(2)}, u32[]{:S(2)}) collective-permute-start(f32[256,768]{1,0:T(8,128)S(1)} %bitcast_add_fusion.1), channel_id=1, source_target_pairs={{0,20},{1,21},{2,22},{3,23},{4,16},{5,17},{6,18},{7,19},{8,28},{9,... | collective-permute-start | bytes 2359304 | tf_op jit(solution)/shard_map/ppermute | solution.py:104
  445.7 17.3 %collective-permute-start.23 = (f32[256,768]{1,0:T(8,128)S(1)}, f32[256,768]{1,0:T(8,128)S(1)}, u32[]{:S(2)}, u32[]{:S(2)}) collective-permute-start(f32[256,768]{1,0:T(8,128)S(1)} %bitcast_add_fusion.4), channel_id=1, source_target_pairs={{0,16},{1,17},{2,18},{3,19},{4,20},{5,21},{6,22},{7,23},{8,24},{9,... | collective-permute-start | bytes 2359304 | tf_op jit(solution)/shard_map/ppermute | solution.py:103
  446.0 19.5 %collective-permute-start.7 = (f32[256,768]{1,0:T(8,128)S(1)}, f32[256,768]{1,0:T(8,128)S(1)}, u32[]{:S(2)}, u32[]{:S(2)}) collective-permute-start(f32[256,768]{1,0:T(8,128)S(1)} %bitcast_add_fusion.7), channel_id=1, source_target_pairs={{0,96},{8,104},{16,112},{24,120},{32,0},{40,8},{48,16},{56,24},{64... | collective-permute-start | bytes 2359304 | tf_op jit(solution)/shard_map/ppermute | solution.py:104
  447.9 17.8 %collective-permute-start.4 = (f32[256,768]{1,0:T(8,128)S(1)}, f32[256,768]{1,0:T(8,128)S(1)}, u32[]{:S(2)}, u32[]{:S(2)}) collective-permute-start(f32[256,768]{1,0:T(8,128)S(1)} %bitcast_add_fusion.10), channel_id=1, source_target_pairs={{0,32},{8,40},{16,48},{24,56},{32,64},{40,72},{48,80},{56,88},{64,... | collective-permute-start | bytes 2359304 | tf_op jit(solution)/shard_map/ppermute | solution.py:103
  463.4 5.7 %collective-permute-start.30 = (f32[64,768]{1,0:T(8,128)S(1)}, f32[64,768]{1,0:T(8,128)S(1)}, u32[]{:S(2)}, u32[]{:S(2)}) collective-permute-start(f32[64,768]{1,0:T(8,128)S(1)} %dynamic-slice_bitcast_fusion.4), channel_id=1, source_target_pairs={{0,3},{1,0},{2,1},{3,2},{4,7},{5,4},{6,5},{7,6},{8,11},{9,8},{10,9... | collective-permute-start | bytes 589832 | tf_op jit(solution)/shard_map/ppermute | solution.py:104
  463.9 7.0 %collective-permute-start.27 = (f32[64,768]{1,0:T(8,128)S(1)}, f32[64,768]{1,0:T(8,128)S(1)}, u32[]{:S(2)}, u32[]{:S(2)}) collective-permute-start(f32[64,768]{1,0:T(8,128)S(1)} %dynamic-slice_bitcast_fusion.5), channel_id=1, source_target_pairs={{0,1},{1,2},{2,3},{3,0},{4,5},{5,6},{6,7},{7,4},{8,9},{9,10},{10,1... | collective-permute-start | bytes 589832 | tf_op jit(solution)/shard_map/ppermute | solution.py:103
  466.0 5.7 %collective-permute-start.11 = (f32[64,768]{1,0:T(8,128)S(1)}, f32[64,768]{1,0:T(8,128)S(1)}, u32[]{:S(2)}, u32[]{:S(2)}) collective-permute-start(f32[64,768]{1,0:T(8,128)S(1)} %dynamic-slice_bitcast_fusion.6), channel_id=1, source_target_pairs={{0,20},{1,21},{2,22},{3,23},{4,16},{5,17},{6,18},{7,19},{8,28},{9,... | collective-permute-start | bytes 589832 | tf_op jit(solution)/shard_map/ppermute | solution.py:104
  466.1 6.9 %collective-permute-start.8 = (f32[64,768]{1,0:T(8,128)S(1)}, f32[64,768]{1,0:T(8,128)S(1)}, u32[]{:S(2)}, u32[]{:S(2)}) collective-permute-start(f32[64,768]{1,0:T(8,128)S(1)} %dynamic-slice_bitcast_fusion.7), channel_id=1, source_target_pairs={{0,16},{1,17},{2,18},{3,19},{4,20},{5,21},{6,22},{7,23},{8,24},{9,... | collective-permute-start | bytes 589832 | tf_op jit(solution)/shard_map/ppermute | solution.py:103
  469.1 5.7 %collective-permute-start.31 = (f32[64,768]{1,0:T(8,128)S(1)}, f32[64,768]{1,0:T(8,128)S(1)}, u32[]{:S(2)}, u32[]{:S(2)}) collective-permute-start(f32[64,768]{1,0:T(8,128)S(1)} %bitcast_add_fusion.20), channel_id=1, source_target_pairs={{0,3},{1,0},{2,1},{3,2},{4,7},{5,4},{6,5},{7,6},{8,11},{9,8},{10,9... | collective-permute-start | bytes 589832 | tf_op jit(solution)/shard_map/ppermute | solution.py:104
  470.9 7.2 %collective-permute-start.28 = (f32[64,768]{1,0:T(8,128)S(1)}, f32[64,768]{1,0:T(8,128)S(1)}, u32[]{:S(2)}, u32[]{:S(2)}) collective-permute-start(f32[64,768]{1,0:T(8,128)S(1)} %bitcast_add_fusion.23), channel_id=1, source_target_pairs={{0,1},{1,2},{2,3},{3,0},{4,5},{5,6},{6,7},{7,4},{8,9},{9,10},{10,1... | collective-permute-start | bytes 589832 | tf_op jit(solution)/shard_map/ppermute | solution.py:103
  471.8 6.4 %collective-permute-start.12 = (f32[64,768]{1,0:T(8,128)S(1)}, f32[64,768]{1,0:T(8,128)S(1)}, u32[]{:S(2)}, u32[]{:S(2)}) collective-permute-start(f32[64,768]{1,0:T(8,128)S(1)} %bitcast_add_fusion.26), channel_id=1, source_target_pairs={{0,20},{1,21},{2,22},{3,23},{4,16},{5,17},{6,18},{7,19},{8,28},{9,... | collective-permute-start | bytes 589832 | tf_op jit(solution)/shard_map/ppermute | solution.py:104
  473.1 6.9 %collective-permute-start.9 = (f32[64,768]{1,0:T(8,128)S(1)}, f32[64,768]{1,0:T(8,128)S(1)}, u32[]{:S(2)}, u32[]{:S(2)}) collective-permute-start(f32[64,768]{1,0:T(8,128)S(1)} %bitcast_add_fusion.29), channel_id=1, source_target_pairs={{0,16},{1,17},{2,18},{3,19},{4,20},{5,21},{6,22},{7,23},{8,24},{9,... | collective-permute-start | bytes 589832 | tf_op jit(solution)/shard_map/ppermute | solution.py:103
  474.9 6.7 %collective-permute-start.32 = (f32[64,768]{1,0:T(8,128)S(1)}, f32[64,768]{1,0:T(8,128)S(1)}, u32[]{:S(2)}, u32[]{:S(2)}) collective-permute-start(f32[64,768]{1,0:T(8,128)S(1)} %bitcast_add_fusion.19), channel_id=1, source_target_pairs={{0,3},{1,0},{2,1},{3,2},{4,7},{5,4},{6,5},{7,6},{8,11},{9,8},{10,9... | collective-permute-start | bytes 589832 | tf_op jit(solution)/shard_map/ppermute | solution.py:104
  478.1 7.5 %collective-permute-start.29 = (f32[64,768]{1,0:T(8,128)S(1)}, f32[64,768]{1,0:T(8,128)S(1)}, u32[]{:S(2)}, u32[]{:S(2)}) collective-permute-start(f32[64,768]{1,0:T(8,128)S(1)} %bitcast_add_fusion.22), channel_id=1, source_target_pairs={{0,1},{1,2},{2,3},{3,0},{4,5},{5,6},{6,7},{7,4},{8,9},{9,10},{10,1... | collective-permute-start | bytes 589832 | tf_op jit(solution)/shard_map/ppermute | solution.py:103
  478.3 9.8 %collective-permute-start.13 = (f32[64,768]{1,0:T(8,128)S(1)}, f32[64,768]{1,0:T(8,128)S(1)}, u32[]{:S(2)}, u32[]{:S(2)}) collective-permute-start(f32[64,768]{1,0:T(8,128)S(1)} %bitcast_add_fusion.25), channel_id=1, source_target_pairs={{0,20},{1,21},{2,22},{3,23},{4,16},{5,17},{6,18},{7,19},{8,28},{9,... | collective-permute-start | bytes 589832 | tf_op jit(solution)/shard_map/ppermute | solution.py:104
  480.1 8.0 %collective-permute-start.10 = (f32[64,768]{1,0:T(8,128)S(1)}, f32[64,768]{1,0:T(8,128)S(1)}, u32[]{:S(2)}, u32[]{:S(2)}) collective-permute-start(f32[64,768]{1,0:T(8,128)S(1)} %bitcast_add_fusion.28), channel_id=1, source_target_pairs={{0,16},{1,17},{2,18},{3,19},{4,20},{5,21},{6,22},{7,23},{8,24},{9,... | collective-permute-start | bytes 589832 | tf_op jit(solution)/shard_map/ppermute | solution.py:103
  488.0 5.6 %collective-permute-start.33 = (f32[16,768]{1,0:T(8,128)S(1)}, f32[16,768]{1,0:T(8,128)S(1)}, u32[]{:S(2)}, u32[]{:S(2)}) collective-permute-start(f32[16,768]{1,0:T(8,128)S(1)} %dynamic-slice_bitcast_fusion.11), channel_id=1, source_target_pairs={{0,32},{8,40},{16,48},{24,56},{32,64},{40,72},{48,80},{56,88},{64,... | collective-permute-start | bytes 147464 | tf_op jit(solution)/shard_map/ppermute | solution.py:103
  488.2 5.5 %collective-permute-start.17 = (f32[16,768]{1,0:T(8,128)S(1)}, f32[16,768]{1,0:T(8,128)S(1)}, u32[]{:S(2)}, u32[]{:S(2)}) collective-permute-start(f32[16,768]{1,0:T(8,128)S(1)} %dynamic-slice_bitcast_fusion.12), channel_id=1, source_target_pairs={{0,3},{1,0},{2,1},{3,2},{4,7},{5,4},{6,5},{7,6},{8,11},{9,8},{10,9... | collective-permute-start | bytes 147464 | tf_op jit(solution)/shard_map/ppermute | solution.py:104
  489.1 6.0 %collective-permute-start.14 = (f32[16,768]{1,0:T(8,128)S(1)}, f32[16,768]{1,0:T(8,128)S(1)}, u32[]{:S(2)}, u32[]{:S(2)}) collective-permute-start(f32[16,768]{1,0:T(8,128)S(1)} %dynamic-slice_bitcast_fusion.13), channel_id=1, source_target_pairs={{0,1},{1,2},{2,3},{3,0},{4,5},{5,6},{6,7},{7,4},{8,9},{9,10},{10,1... | collective-permute-start | bytes 147464 | tf_op jit(solution)/shard_map/ppermute | solution.py:103
  490.3 5.6 %collective-permute-start.37 = (f32[16,768]{1,0:T(8,128)S(1)}, f32[16,768]{1,0:T(8,128)S(1)}, u32[]{:S(2)}, u32[]{:S(2)}) collective-permute-start(f32[16,768]{1,0:T(8,128)S(1)} %bitcast_add_fusion.38), channel_id=1, source_target_pairs={{0,96},{8,104},{16,112},{24,120},{32,0},{40,8},{48,16},{56,24},{64... | collective-permute-start | bytes 147464 | tf_op jit(solution)/shard_map/ppermute | solution.py:104
  493.6 5.6 %collective-permute-start.34 = (f32[16,768]{1,0:T(8,128)S(1)}, f32[16,768]{1,0:T(8,128)S(1)}, u32[]{:S(2)}, u32[]{:S(2)}) collective-permute-start(f32[16,768]{1,0:T(8,128)S(1)} %bitcast_add_fusion.41), channel_id=1, source_target_pairs={{0,32},{8,40},{16,48},{24,56},{32,64},{40,72},{48,80},{56,88},{64,... | collective-permute-start | bytes 147464 | tf_op jit(solution)/shard_map/ppermute | solution.py:103
  493.7 5.6 %collective-permute-start.18 = (f32[16,768]{1,0:T(8,128)S(1)}, f32[16,768]{1,0:T(8,128)S(1)}, u32[]{:S(2)}, u32[]{:S(2)}) collective-permute-start(f32[16,768]{1,0:T(8,128)S(1)} %bitcast_add_fusion.44), channel_id=1, source_target_pairs={{0,3},{1,0},{2,1},{3,2},{4,7},{5,4},{6,5},{7,6},{8,11},{9,8},{10,9... | collective-permute-start | bytes 147464 | tf_op jit(solution)/shard_map/ppermute | solution.py:104
  495.1 6.8 %collective-permute-start.15 = (f32[16,768]{1,0:T(8,128)S(1)}, f32[16,768]{1,0:T(8,128)S(1)}, u32[]{:S(2)}, u32[]{:S(2)}) collective-permute-start(f32[16,768]{1,0:T(8,128)S(1)} %bitcast_add_fusion.47), channel_id=1, source_target_pairs={{0,1},{1,2},{2,3},{3,0},{4,5},{5,6},{6,7},{7,4},{8,9},{9,10},{10,1... | collective-permute-start | bytes 147464 | tf_op jit(solution)/shard_map/ppermute | solution.py:103
  495.9 6.1 %collective-permute-start.38 = (f32[16,768]{1,0:T(8,128)S(1)}, f32[16,768]{1,0:T(8,128)S(1)}, u32[]{:S(2)}, u32[]{:S(2)}) collective-permute-start(f32[16,768]{1,0:T(8,128)S(1)} %bitcast_add_fusion.37), channel_id=1, source_target_pairs={{0,96},{8,104},{16,112},{24,120},{32,0},{40,8},{48,16},{56,24},{64... | collective-permute-start | bytes 147464 | tf_op jit(solution)/shard_map/ppermute | solution.py:104
  499.2 5.4 %collective-permute-start.35 = (f32[16,768]{1,0:T(8,128)S(1)}, f32[16,768]{1,0:T(8,128)S(1)}, u32[]{:S(2)}, u32[]{:S(2)}) collective-permute-start(f32[16,768]{1,0:T(8,128)S(1)} %bitcast_add_fusion.40), channel_id=1, source_target_pairs={{0,32},{8,40},{16,48},{24,56},{32,64},{40,72},{48,80},{56,88},{64,... | collective-permute-start | bytes 147464 | tf_op jit(solution)/shard_map/ppermute | solution.py:103
  501.9 5.4 %collective-permute-start.16 = (f32[16,768]{1,0:T(8,128)S(1)}, f32[16,768]{1,0:T(8,128)S(1)}, u32[]{:S(2)}, u32[]{:S(2)}) collective-permute-start(f32[16,768]{1,0:T(8,128)S(1)} %bitcast_add_fusion.46), channel_id=1, source_target_pairs={{0,1},{1,2},{2,3},{3,0},{4,5},{5,6},{6,7},{7,4},{8,9},{9,10},{10,1... | collective-permute-start | bytes 147464 | tf_op jit(solution)/shard_map/ppermute | solution.py:103
  (39 other events, 623.0 us)
